TPU v7x, 256 devices: a whole 4x4x8 slice. The times are simulated.
256 devices in a mesh: space: 32 (over z, x), mode: 8 (over y, core).
Axes of the slice: x: 4, y: 4, z: 8, core: 2. Of those that a mesh axis runs over, the one named last changes fastest.
Arguments:
- vectors: float32 [55296, 256], P('space', 'mode'), may hold values from -6 to 6
- force_blocks: float32 [288, 27, 192, 192], P('space', None, 'mode'), as said below
- inverse_blocks: float32 [288, 192, 192], P('space'), as said below
- neighbours: int32 [288, 27], P('space'), may hold values from 0 to 287, as said below
Outputs:
- w_block: float32 [55296, 256], P('space', 'mode')
- hw_block: float32 [55296, 256], P('space', 'mode')
- gram_a: float32 [512, 2, 256], P(None, None, 'mode')
- gram_b: float32 [512, 2, 256], P(None, None, 'mode')
Inputs may be any that keep to these rules, and one draw needn't show every extreme that they name: `neighbours`: block rows are atom cells on a periodic grid of 32 layers of 3 x 3 cells; the rows of layer z are z * 9 to z * 9 + 8 in some order. Entry k = 9 (dz + 1) + 3 (dy + 1) + (dx + 1) of row i is the block row of the cell at offset (dz, dy, dx) from row i's cell, so entry 13 is i itself. H is symmetric: force_blocks[neighbours[i, k], 26 - k] is the transpose of force_blocks[i, k]. `inverse_blocks`: every block is symmetric.
All inputs are finite; a program needn't handle non-finite values.
Results may differ from a plain program's by a relative error of at most 0.00013.
Values sent between devices are 32-bit elements; how exact they have to be, the bound alone decides.
No kernel may reach another device: no remote copies, remote signals or barrier semaphores. Data moves between devices by JAX's collectives and lax.ppermute only.
A program may use at most 128 MiB of HBM per device.

v0:
```python
import jax
import jax.numpy as jnp
from jax import lax
from jax.sharding import PartitionSpec as P

CELLS = 9


def extended_2(block, sides, width):
    for axis, dim in sides:
        count = lax.axis_size(axis)
        forward = [(i, i + 1) for i in range(count - 1)]
        forward.append((count - 1, 0))
        backward = [(target, source) for source, target in forward]
        low = lax.ppermute(
            lax.slice_in_dim(block, block.shape[dim] - width, None, axis=dim), axis, forward
        )
        high = lax.ppermute(lax.slice_in_dim(block, 0, width, axis=dim), axis, backward)
        block = jnp.concatenate([low, block, high], axis=dim)
    return block


def apply_local(force_blocks, local_ids, extended):

    def accumulate(totals, offset):
        gathered = jnp.take(extended, local_ids[:, offset], axis=0)
        force_slice = lax.dynamic_index_in_dim(force_blocks, offset, 1, keepdims=False)
        product = jnp.einsum(
            "brc,bcm->brm",
            force_slice,
            gathered,
            precision=lax.Precision.HIGHEST,
            preferred_element_type=jnp.float32,
        )
        return (totals + product, None)

    initial = jnp.zeros(
        (force_blocks.shape[0], force_blocks.shape[2], extended.shape[2]), jnp.float32
    )
    totals, unused = lax.scan(
        accumulate, initial, jnp.arange(force_blocks.shape[1], dtype=jnp.int32)
    )
    regrouped = lax.all_to_all(totals, "mode", split_axis=2, concat_axis=1, tiled=True)
    return regrouped.reshape(-1, regrouped.shape[2])


def spread_search(search_field):
    gathered = lax.all_gather(search_field, "mode", axis=2, tiled=True)
    extended = extended_2(gathered, (("space", 0),), CELLS)
    return (gathered, extended)


def local_gram(flat_x, full_w, vectors, w_local, image_x, image_w, total_rows):
    basis = jnp.concatenate([flat_x, full_w.reshape(flat_x.shape)], axis=1)
    columns = jnp.stack([vectors, w_local, image_x, image_w], axis=1)
    return (
        jnp.einsum(
            "ra,rgj->agj",
            basis,
            columns,
            precision=lax.Precision.HIGHEST,
            preferred_element_type=jnp.float32,
        )
        / total_rows
    )


def local(vectors, force_blocks, inverse_blocks, neighbours):
    row_count, col_count = vectors.shape
    block_size = inverse_blocks.shape[1]
    block_rows = row_count // block_size
    slab_count = lax.axis_size("space")
    total_rows = row_count * slab_count
    own_layers = block_rows // CELLS
    layer_total = own_layers * slab_count
    slab_index = lax.axis_index("space")
    layer_of = neighbours // CELLS
    relative = (layer_of - slab_index * own_layers + 1) % layer_total
    local_ids = relative * CELLS + neighbours % CELLS
    stacked_x = vectors.reshape(block_rows, block_size, col_count)
    full_x = lax.all_gather(stacked_x, "mode", axis=2, tiled=True)
    extended_x = extended_2(full_x, (("space", 0),), CELLS)
    mode_count = full_x.shape[2]
    image_x = apply_local(force_blocks, local_ids, extended_x)
    flat_x = full_x.reshape(row_count, mode_count)
    rayleigh = lax.psum(
        jnp.einsum(
            "ra,rj->aj",
            flat_x,
            image_x,
            precision=lax.Precision.HIGHEST,
            preferred_element_type=jnp.float32,
        )
        / total_rows,
        "space",
    )
    residual = image_x - jnp.dot(
        flat_x, rayleigh, precision=lax.Precision.HIGHEST, preferred_element_type=jnp.float32
    )
    search_raw = jnp.einsum(
        "brc,bcm->brm",
        inverse_blocks,
        residual.reshape(block_rows, block_size, col_count),
        precision=lax.Precision.HIGHEST,
        preferred_element_type=jnp.float32,
    )
    squares = lax.psum(jnp.sum(search_raw * search_raw, axis=(0, 1)), "space")
    scales = lax.rsqrt(squares / total_rows + 1e-06)
    search_field = search_raw * scales
    full_w, extended_w = spread_search(search_field)
    hw_block = apply_local(force_blocks, local_ids, extended_w)
    w_block = search_field.reshape(row_count, col_count)
    gram_sum = lax.psum(
        local_gram(flat_x, full_w, vectors, w_block, image_x, hw_block, total_rows), "space"
    )
    gram_b = gram_sum[:, 0:2]
    gram_a = gram_sum[:, 2:4]
    return (w_block, hw_block, gram_a, gram_b)


def solution(mesh):
    in_specs = (
        P("space", "mode"),
        P("space", None, "mode", None),
        P("space", None, None),
        P("space", None),
    )
    out_specs = (
        P("space", "mode"),
        P("space", "mode"),
        P(None, None, "mode"),
        P(None, None, "mode"),
    )
    return jax.shard_map(local, mesh=mesh, in_specs=in_specs, out_specs=out_specs, check_vma=False)
```

profile of v0, /device:TPU:2, one launch (start us, length us, event | category | flops | bytes accessed | tf_op | source)
XLA Modules:
  0.0 1126.8 jit_solution(3499977427174082303)
XLA Ops:
  9.4 31.6 %all-gather.3.cloned.1.call-done = f32[9,192,256]{1,2,0:T(8,128)} async-done(((f32[9,192,32]{1,2,0:T(8,128)}), f32[9,192,256]{1,2,0:T(8,128)}) %all-gather.3.cloned.1.call-update) | async-done | bytes 1769488 | tf_op jit(solution)/shard_map/all_gather | solution.py:81
  45.9 5.7 copy.80
  52.2 31.7 %collective-permute-done.1 = f32[9,192,256]{2,1,0:T(8,128)} collective-permute-done((f32[9,192,256]{2,1,0:T(8,128)S(1)}, f32[9,192,256]{2,1,0:T(8,128)}, u32[]{:S(2)}, u32[]{:S(2)}) %collective-permute-start.1) | collective-permute-done | bytes 1769504 | tf_op jit(solution)/shard_map/ppermute | solution.py:18
  90.9 5.2 pad_maximum_fusion
  96.1 7.6 copy.81
  103.7 248.9 %while.22 = (s32[]{:T(128)}, f32[9,24,256]{2,1,0:T(8,128)}, s32[27]{0:T(128)S(1)}, f32[9,27,24,192]{3,2,0,1:T(8,128)}, s32[9,27]{0,1:T(8,128)}, /*index=5*/f32[2...) while((s32[]{:T(128)}, f32[9,24,256]{2,1,0:T(8,128)}, s32[27]{0:T(128)S(1)}, ...), condition=%wide.region_1.3_spmd.clone, body=%wide.region_0.2_spmd.clone.sunk | while | flops 127956024 | bytes 5976391 | solution.py:40
  116.1 3.2 gather_fusion
  189.8 3.2 gather_fusion
  352.6 3.4 copy.82
  358.4 10.4 all_to_all.30
  372.4 3.5 copy.104
  380.6 140.5 %psum.21 = f32[256,32]{0,1:T(8,128)} all-reduce(f32[256,32]{0,1:T(8,128)} %fusion.27), channel_id=1, replica_groups=mesh['space'=32,'mode'=8] {'space'}, use_global_device_ids=true, to_apply=%region_2.4 | all-reduce | flops 8192 | bytes 65536 | tf_op jit(solution)/shard_map/psum | solution.py:86
  521.2 3.3 fusion.26
  526.3 3.6 multiply_reduce_fusion
  529.9 75.2 %psum.22 = f32[32]{0:T(128)S(1)} all-reduce(f32[32]{0:T(128)S(1)} %get-tuple-element.203), channel_id=1, replica_groups=mesh['space'=32,'mode'=8] {'space'}, use_global_device_ids=true, to_apply=%region_4.6 | all-reduce | flops 32 | bytes 256 | tf_op jit(solution)/shard_map/psum | solution.py:107
  606.9 24.6 %all-gather.5.cloned.1.call-done = f32[9,192,256]{1,2,0:T(8,128)} async-done(((f32[9,192,32]{1,2,0:T(8,128)}), f32[9,192,256]{1,2,0:T(8,128)}) %all-gather.5.cloned.1.call-update) | async-done | bytes 1769488 | tf_op jit(solution)/shard_map/all_gather | solution.py:48
  635.7 38.8 %collective-permute-done.3 = f32[9,192,256]{2,1,0:T(8,128)} collective-permute-done((f32[9,192,256]{2,1,0:T(8,128)S(1)}, f32[9,192,256]{2,1,0:T(8,128)}, u32[]{:S(2)}, u32[]{:S(2)}) %collective-permute-start.3) | collective-permute-done | bytes 1769504 | tf_op jit(solution)/shard_map/ppermute | solution.py:18
  681.4 5.2 pad_maximum_fusion.1
  686.7 7.6 copy.92
  694.3 248.9 %while.23 = (s32[]{:T(128)}, f32[9,24,256]{2,1,0:T(8,128)}, s32[27]{0:T(128)S(1)}, f32[9,27,24,192]{3,2,0,1:T(8,128)}, s32[9,27]{0,1:T(8,128)}, /*index=5*/f32[2...) while((s32[]{:T(128)}, f32[9,24,256]{2,1,0:T(8,128)}, s32[27]{0:T(128)S(1)}, ...), condition=%wide.region_6.8_spmd.clone, body=%wide.region_5.7_spmd.clone.sunk | while | flops 127956024 | bytes 5976391 | solution.py:40
  943.1 3.5 copy.93
  949.8 4.0 all-to-all-start.1
  955.5 5.4 all-to-all-done.1
  976.8 141.8 %all-reduce.2.cloned.1.call-done = f32[512,4,32]{0,2,1:T(8,128)} async-done(((f32[512,4,32]{0,2,1:T(8,128)}), f32[512,4,32]{0,2,1:T(8,128)}) %all-reduce.2.cloned.1.call-update) | async-done | bytes 262160 | tf_op jit(solution)/shard_map/psum | solution.py:113
  (341 shorter events, 448.4 us)
Async XLA Ops:
  7.2 519.1 %copy-start = (f32[9,192,192]{2,1,0:T(8,128)S(1)}, f32[9,192,192]{2,1,0:T(8,128)}, u32[]{:S(2)}) copy-start(f32[9,192,192]{2,1,0:T(8,128)} %param.12) | copy-start | bytes 3981316
  7.2 33.8 %all-gather.3.cloned.1.call-start = ((), (), s32[]{:S(2)}) async-start(), calls=%async_computation.2 | async-start | bytes 2654208 | tf_op jit(solution)/shard_map/all_gather | solution.py:81
  9.3 622.2 %all-gather.5.cloned.1.call-start = ((), (), s32[]{:S(2)}) async-start(), calls=%async_computation.3 | async-start | bytes 2654208 | tf_op jit(solution)/shard_map/all_gather | solution.py:48
  43.0 8.6 copy-start.2
  43.0 40.9 %collective-permute-start.1 = (f32[9,192,256]{2,1,0:T(8,128)S(1)}, f32[9,192,256]{2,1,0:T(8,128)}, u32[]{:S(2)}, u32[]{:S(2)}) collective-permute-start(f32[9,192,256]{2,1,0:T(8,128)S(1)} %copy.76), channel_id=1, source_target_pairs={{8,0},{16,8},{24,16},{32,24},{40,32},{48,40},{56,48},{64,56},{72,6... | collective-permute-start | bytes 5308424 | tf_op jit(solution)/shard_map/ppermute | solution.py:18
  43.7 44.3 %collective-permute-start = (f32[9,192,256]{2,1,0:T(8,128)S(1)}, f32[9,192,256]{2,1,0:T(8,128)}, u32[]{:S(2)}, u32[]{:S(2)}) collective-permute-start(f32[9,192,256]{2,1,0:T(8,128)S(1)} %copy.76), channel_id=1, source_target_pairs={{0,8},{8,16},{16,24},{24,32},{32,40},{40,48},{48,56},{56,64},{64,7... | collective-permute-start | bytes 5308424 | tf_op jit(solution)/shard_map/ppermute | solution.py:15
  372.4 5.8 copy-start.3
  633.6 47.9 %copy-start.7 = (f32[9,192,256]{2,1,0:T(8,128)}, f32[9,192,256]{2,1,0:T(8,128)S(1)}, u32[]{:S(2)}) copy-start(f32[9,192,256]{2,1,0:T(8,128)S(1)} %copy.87) | copy-start | bytes 5308420
  633.6 40.9 %collective-permute-start.3 = (f32[9,192,256]{2,1,0:T(8,128)S(1)}, f32[9,192,256]{2,1,0:T(8,128)}, u32[]{:S(2)}, u32[]{:S(2)}) collective-permute-start(f32[9,192,256]{2,1,0:T(8,128)S(1)} %copy.87), channel_id=1, source_target_pairs={{8,0},{16,8},{24,16},{32,24},{40,32},{48,40},{56,48},{64,56},{72,6... | collective-permute-start | bytes 5308424 | tf_op jit(solution)/shard_map/ppermute | solution.py:18
  634.2 44.3 %collective-permute-start.2 = (f32[9,192,256]{2,1,0:T(8,128)S(1)}, f32[9,192,256]{2,1,0:T(8,128)}, u32[]{:S(2)}, u32[]{:S(2)}) collective-permute-start(f32[9,192,256]{2,1,0:T(8,128)S(1)} %copy.87), channel_id=1, source_target_pairs={{0,8},{8,16},{16,24},{24,32},{32,40},{40,48},{48,56},{56,64},{64,7... | collective-permute-start | bytes 5308424 | tf_op jit(solution)/shard_map/ppermute | solution.py:15
  943.1 10.9 copy-start.4
  946.6 8.5 copy-start.10
  949.8 11.1 all-to-all-start.1
  953.8 164.8 %all-reduce.2.cloned.1.call-start = ((), (), s32[]{:S(2)}) async-start(), calls=%async_computation.4 | async-start | bytes 524288 | tf_op jit(solution)/shard_map/psum | solution.py:113
  955.3 9.5 copy-start.9
  964.8 4.4 copy-start.11
  967.2 1.0 copy-start.5
  969.3 1.7 copy-start.8
  970.9 149.4 %copy-start.1 = (f32[9,192,192]{2,1,0:T(8,128)S(1)}, f32[9,192,192]{2,1,0:T(8,128)}, u32[]{:S(2)}) copy-start(f32[9,192,192]{2,1,0:T(8,128)} %param.12) | copy-start | bytes 3981316
  973.2 2.6 copy-start.6
Sparse Core Ops, SparseCore 0:
  9.8 31.0 all-gather.2
  607.0 24.4 all-gather.4
  974.0 144.5 all-reduce.1
where the time goes:
time: 1140 us; the launch traced here: 1130 us
  local copies, waits for them, and re-layouts  277 us (24%)
  waiting for transfers between devices  276 us (24%)
  blocking collectives  226 us (20%)
  matrix products  163 us (14%)
  loops' own time  106 us (9%)
  other arithmetic  56.2 us (5%)
  between operations  13.9 us (1%)
    gather x54, local copies, waits for them, and re-layouts, accumulate(): gathered = jnp.take(extended, local_ids[:, offset], axis=0)  171 us
    dot_general x54, matrix products, accumulate(): jnp.einsum('brc,bcm->brm', force_slice, gathered, precision=lax.Precision...  152 us
    psum x1, waiting for transfers between devices, local(): lax.psum(local_gram(flat_x, full_w, vectors, w_block, image_x, hw_block,...  142 us
    psum x1, blocking collectives, local(): lax.psum(jnp.einsum('ra,rj->aj', flat_x, image_x, precision=lax.Precision...  141 us
    another operation x2, loops' own time, apply_local(): lax.scan(accumulate, initial, jnp.arange(force_blocks.shape[1], dtype=jnp...  106 us
    psum x1, blocking collectives, local(): squares = lax.psum(jnp.sum(search_raw * search_raw, axis=(0, 1)), 'space')  75.2 us
    ppermute x2, waiting for transfers between devices, extended_2(): lax.ppermute(lax.slice_in_dim(block, 0, width, axis=dim), axis, backward)  70.5 us
    and x54, other arithmetic, accumulate(): gathered = jnp.take(extended, local_ids[:, offset], axis=0)  37.9 us
  transfers between devices with their start and end apart: 8, of which 8 were waited for; matrix products, arithmetic and copies ran while one was open for 2% of the time, Pallas kernels for 0%

commit v1 on v0

v1 whole, which is shorter than its diff:
```python
import jax
import jax.numpy as jnp
from jax import lax
from jax.sharding import PartitionSpec as P

CELLS = 9
HIGHEST = lax.Precision.HIGHEST


def space_sum(value):
    count = lax.axis_size("space")
    step = 1
    while step < count:
        pairs = [(i, i ^ step) for i in range(count)]
        value = value + lax.ppermute(value, "space", pairs)
        step *= 2
    return value


def halo(block, width):
    count = lax.axis_size("space")
    forward = [(i, (i + 1) % count) for i in range(count)]
    backward = [((i + 1) % count, i) for i in range(count)]
    low = lax.ppermute(block[block.shape[0] - width :], "space", forward)
    high = lax.ppermute(block[:width], "space", backward)
    return low, high


def dense_rows(force_blocks, local_ids, ext_blocks):
    block_rows, neigh = local_ids.shape
    columns = jnp.arange(ext_blocks, dtype=jnp.int32)
    onehot = local_ids[:, :, None] == columns[None, None, :]
    offsets = jnp.arange(neigh, dtype=jnp.int32)
    which = jnp.sum(jnp.where(onehot, offsets[None, :, None], 0), axis=1)
    valid = jnp.any(onehot, axis=1)
    flat = (jnp.arange(block_rows, dtype=jnp.int32)[:, None] * neigh + which).reshape(-1)
    rows, cols = force_blocks.shape[2], force_blocks.shape[3]
    table = force_blocks.reshape(block_rows * neigh, rows * cols)
    picked = jnp.take(table, flat, axis=0).reshape(block_rows, ext_blocks, rows, cols)
    return jnp.where(valid[:, :, None, None], picked, 0.0)


def apply_dense(dense, low, own, high):
    width = low.shape[0]
    own_count = own.shape[0]
    parts = (
        (dense[:, width : width + own_count], own),
        (dense[:, :width], low),
        (dense[:, width + own_count :], high),
    )
    total = None
    for coeffs, field in parts:
        product = jnp.einsum(
            "ijrc,jcm->irm",
            coeffs,
            field,
            precision=HIGHEST,
            preferred_element_type=jnp.float32,
        )
        total = product if total is None else total + product
    regrouped = lax.all_to_all(total, "mode", split_axis=2, concat_axis=1, tiled=True)
    return regrouped.reshape(-1, regrouped.shape[2])


def local(vectors, force_blocks, inverse_blocks, neighbours):
    row_count, col_count = vectors.shape
    block_size = inverse_blocks.shape[1]
    block_rows = row_count // block_size
    slab_count = lax.axis_size("space")
    total_rows = row_count * slab_count
    own_layers = block_rows // CELLS
    layer_total = own_layers * slab_count
    slab_index = lax.axis_index("space")
    mode_index = lax.axis_index("mode")
    layer_of = neighbours // CELLS
    relative = (layer_of - slab_index * own_layers + 1) % layer_total
    local_ids = relative * CELLS + neighbours % CELLS
    ext_blocks = block_rows + 2 * CELLS
    dense = dense_rows(force_blocks, local_ids, ext_blocks)

    stacked_x = vectors.reshape(block_rows, block_size, col_count)
    full_x = lax.all_gather(stacked_x, "mode", axis=2, tiled=True)
    low_x, high_x = halo(full_x, CELLS)
    image_x = apply_dense(dense, low_x, full_x, high_x)
    mode_count = full_x.shape[2]
    flat_x = full_x.reshape(row_count, mode_count)
    rayleigh = (
        space_sum(
            jnp.einsum(
                "ra,rj->aj",
                flat_x,
                image_x,
                precision=HIGHEST,
                preferred_element_type=jnp.float32,
            )
        )
        / total_rows
    )
    residual = image_x - jnp.dot(
        flat_x, rayleigh, precision=HIGHEST, preferred_element_type=jnp.float32
    )
    search_raw = jnp.einsum(
        "brc,bcm->brm",
        inverse_blocks,
        residual.reshape(block_rows, block_size, col_count),
        precision=HIGHEST,
        preferred_element_type=jnp.float32,
    )
    full_s = lax.all_gather(search_raw, "mode", axis=2, tiled=True)
    low_s, high_s = halo(full_s, CELLS)
    image_s = apply_dense(dense, low_s, full_s, high_s)
    flat_s = full_s.reshape(row_count, mode_count)
    own_s = search_raw.reshape(row_count, col_count)

    squares = jnp.sum(flat_s * flat_s, axis=0)
    basis = jnp.concatenate([flat_x, flat_s], axis=1)
    columns = jnp.stack([vectors, own_s, image_x, image_s], axis=1)
    gram_part = jnp.einsum(
        "ra,rgj->agj", basis, columns, precision=HIGHEST, preferred_element_type=jnp.float32
    )
    packed = jnp.concatenate([gram_part.reshape(-1), squares])
    summed = space_sum(packed)
    gram_sum = summed[: gram_part.size].reshape(gram_part.shape)
    scales_all = lax.rsqrt(summed[gram_part.size :] / total_rows + 1e-06)
    scales_own = lax.dynamic_slice_in_dim(scales_all, mode_index * col_count, col_count)

    w_block = own_s * scales_own
    hw_block = image_s * scales_own
    row_scale = jnp.concatenate([jnp.ones((mode_count,), jnp.float32), scales_all])
    ones_own = jnp.ones((col_count,), jnp.float32)
    col_scale = jnp.stack([ones_own, scales_own, ones_own, scales_own])
    gram = gram_sum * row_scale[:, None, None] * col_scale[None] / total_rows
    gram_b = gram[:, 0:2]
    gram_a = gram[:, 2:4]
    return (w_block, hw_block, gram_a, gram_b)


def solution(mesh):
    in_specs = (
        P("space", "mode"),
        P("space", None, "mode", None),
        P("space", None, None),
        P("space", None),
    )
    out_specs = (
        P("space", "mode"),
        P("space", "mode"),
        P(None, None, "mode"),
        P(None, None, "mode"),
    )
    return jax.shard_map(local, mesh=mesh, in_specs=in_specs, out_specs=out_specs, check_vma=False)
```

time: 1140 us -> 347 us (0.30)
  blocking collectives: 226 us -> 11.1 us
  local copies, waits for them, and re-layouts: 277 us -> 68.1 us
  matrix products: 163 us -> 39.1 us
  waiting for transfers between devices: 276 us -> 165 us
  loops' own time: 106 us -> 0 us
  other arithmetic: 56.2 us -> 12.6 us
  starting transfers between devices: 8.57 us -> 30.4 us
    psum x2 -> x0, blocking collectives: 216 us -> none  [the longest x1 141 us: local(): lax.psum(jnp.einsum('ra,rj->aj', flat_x, image_x, precision=lax.Precision...]
    gather x54 -> x2, local copies, waits for them, and re-layouts: 171 us -> 14.9 us  [dense_rows(): jnp.take(table, flat, axis=0).reshape(block_rows, ext_blocks, rows, cols)]
    psum x1 -> x0, waiting for transfers between devices: 142 us -> none  [local(): lax.psum(local_gram(flat_x, full_w, vectors, w_block, image_x, hw_block,...]
    dot_general x56 -> x8, matrix products: 157 us -> 29.3 us  [the longest x6 25.1 us: apply_dense(): jnp.einsum('ijrc,jcm->irm', coeffs, field, precision=HIGHEST, preferred_e...]
    another operation x2 -> x0, loops' own time: 106 us -> none  [apply_local(): lax.scan(accumulate, initial, jnp.arange(force_blocks.shape[1], dtype=jnp...]
    and x54 -> x1, other arithmetic: 37.9 us -> 0.67 us  [dense_rows(): jnp.take(table, flat, axis=0).reshape(block_rows, ext_blocks, rows, cols)]
    dynamic_slice x54 -> x1, local copies, waits for them, and re-layouts: 31.4 us -> 0.07 us  [local(): lax.dynamic_slice_in_dim(scales_all, mode_index * col_count, col_count)]
    ppermute x4 -> x14, waiting for transfers between devices: 72.6 us -> 101 us  [the longest x10 60.5 us: space_sum(): value = value + lax.ppermute(value, 'space', pairs)]
  transfers between devices with their start and end apart: 8 -> 17, of which waited for: 8 -> 15; matrix products, arithmetic and copies ran while one was open for 2% -> 14% of each run, Pallas kernels for 0% -> 0%
where the time goes in v1:
time: 347 us; the launch traced here: 341 us
  waiting for transfers between devices  165 us (48%)
  local copies, waits for them, and re-layouts  68.1 us (20%)
  matrix products  39.1 us (11%)
  starting transfers between devices  30.4 us (9%)
  between operations  14.6 us (4%)
  other arithmetic  12.6 us (4%)
  blocking collectives  11.1 us (3%)
    ppermute x10, waiting for transfers between devices, space_sum(): value = value + lax.ppermute(value, 'space', pairs)  60.5 us
    ppermute x2, waiting for transfers between devices, halo(): low = lax.ppermute(block[block.shape[0] - width:], 'space', forward)  40.7 us
    all_gather x1, waiting for transfers between devices, local(): full_x = lax.all_gather(stacked_x, 'mode', axis=2, tiled=True)  31.6 us
    all_gather x1, waiting for transfers between devices, local(): full_s = lax.all_gather(search_raw, 'mode', axis=2, tiled=True)  26.8 us
    dot_general x6, matrix products, apply_dense(): jnp.einsum('ijrc,jcm->irm', coeffs, field, precision=HIGHEST, preferred_e...  25.1 us
    ppermute x10, starting transfers between devices, space_sum(): value = value + lax.ppermute(value, 'space', pairs)  22 us
    gather x2, local copies, waits for them, and re-layouts, dense_rows(): jnp.take(table, flat, axis=0).reshape(block_rows, ext_blocks, rows, cols)  14.9 us
    unnamed x32, local copies, waits for them, and re-layouts  12.6 us
  transfers between devices with their start and end apart: 17, of which 15 were waited for; matrix products, arithmetic and copies ran while one was open for 14% of the time, Pallas kernels for 0%

profile of v1, /device:TPU:2, one launch (start us, length us, event | category | flops | bytes accessed | tf_op | source)
XLA Modules:
  0.0 340.6 jit_solution(18224668722310381705)
XLA Ops:
  9.4 31.6 %all-gather.3.cloned.1.call-done = f32[9,192,256]{1,2,0:T(8,128)} async-done(((f32[9,192,32]{1,2,0:T(8,128)}), f32[9,192,256]{1,2,0:T(8,128)}) %all-gather.3.cloned.1.call-update) | async-done | bytes 1769488 | tf_op jit(solution)/shard_map/all_gather | solution.py:82
  46.7 6.7 %reshape.102 = f32[243,4608]{1,0:T(8,128)} reshape(f32[9,27,24,192]{3,2,1,0:T(8,128)} %param.5) | data formatting | bytes 8957952 | tf_op jit(solution)/shard_map/reshape | solution.py:38
  53.5 8.4 %gather_fusion = f32[243,4608]{1,0:T(8,128)} fusion(f32[243,4608]{1,0:T(8,128)} %reshape.102, s32[1024]{0:T(1024)S(1)} %pad_clamp_fusion), kind=kCustom, calls=%fused_computation | custom fusion | bytes 8958924 | tf_op jit(solution)/shard_map/jit(_take)/gather | solution.py:39
  61.9 6.5 %gather.7 = f32[9,27,24,192]{3,2,1,0:T(8,128)} reshape(f32[243,4608]{1,0:T(8,128)} %gather_fusion) | data formatting | bytes 8957952 | tf_op jit(solution)/shard_map/jit(_take)/gather | solution.py:39
  68.5 4.6 %fusion.19 = f32[9,24,256]{2,1,0:T(8,128)S(1)} fusion(f32[9,192,256]{1,2,0:T(8,128)} %all-gather.3.cloned.1.call-done, f32[9,27,24,192]{3,2,1,0:T(8,128)} %gather.7, pred[9,27]{1,0:T(8,128)(4,1)S(1)} %get-tuple-element.16, pred[9,27]{1,0:T(8,128)(4,1)S(1)} %fusion.47), kind=kOutput, calls=%fused_computation.25 | convolution fusion | flops 1148857344 | bytes 6470118 | tf_op jit(solution)/shard_map/ijrc,jcm->irm/dot_general | solution.py:53
  73.2 10.8 %collective-permute-done = f32[9,192,256]{2,1,0:T(8,128)} collective-permute-done((f32[9,192,256]{2,1,0:T(8,128)S(1)}, f32[9,192,256]{2,1,0:T(8,128)}, u32[]{:S(2)}, u32[]{:S(2)}) %collective-permute-start) | collective-permute-done | bytes 1769504 | tf_op jit(solution)/shard_map/ppermute | solution.py:24
  87.4 4.2 %fusion.34 = f32[9,24,256]{2,1,0:T(8,128)} fusion(f32[9,24,256]{2,1,0:T(8,128)S(1)} %fusion.37, f32[9,192,256]{2,1,0:T(8,128)} %collective-permute-done.1, f32[9,27,24,192]{3,2,1,0:T(8,128)S(1)} %copy-done.1, pred[9,27]{1,0:T(8,128)(4,1)S(1)} %get-tuple-element.16, pred[9,27]{1,0:T(8,128)(4,1)S(1)} %fusion.47), kind=kOutput, calls=%fused_computation.30 | convolution fusion | flops 1148912640 | bytes 6691302 | tf_op jit(solution)/shard_map/ijrc,jcm->irm/dot_general | solution.py:53
  98.1 11.1 %all_to_all.30 = f32[8,1,6912]{2,1,0:T(1,128)} all-to-all(f32[8,1,6912]{2,1,0:T(1,128)} %reshape.133), channel_id=1, replica_groups=mesh['space'=32,'mode'=8] {'mode'}, dimensions={0} | all-to-all | bytes 442368 | tf_op jit(solution)/shard_map/all_to_all | solution.py:61
  122.8 4.3 %collective-permute-start.2 = (f32[256,32]{0,1:T(8,128)S(1)}, f32[256,32]{0,1:T(8,128)S(1)}, u32[]{:S(2)}, u32[]{:S(2)}) collective-permute-start(f32[256,32]{0,1:T(8,128)S(1)} %convolution_bitcast_fusion.3), channel_id=1, source_target_pairs={{0,8},{8,0},{16,24},{24,16},{32,40},{40,32},{48,56},{56,48},{64,72... | collective-permute-start | bytes 98312 | tf_op jit(solution)/shard_map/ppermute | solution.py:15
  129.1 5.4 %collective-permute-done.3 = f32[256,32]{0,1:T(8,128)S(1)} collective-permute-done((f32[256,32]{0,1:T(8,128)S(1)}, f32[256,32]{0,1:T(8,128)S(1)}, u32[]{:S(2)}, u32[]{:S(2)}) %collective-permute-start.3) | collective-permute-done | bytes 32800 | tf_op jit(solution)/shard_map/ppermute | solution.py:15
  143.4 5.4 %collective-permute-start.6 = (f32[256,32]{0,1:T(8,128)S(1)}, f32[256,32]{0,1:T(8,128)S(1)}, u32[]{:S(2)}, u32[]{:S(2)}) collective-permute-start(f32[256,32]{0,1:T(8,128)S(1)} %add.131), channel_id=1, source_target_pairs={{0,128},{8,136},{16,144},{24,152},{32,160},{40,168},{48,176},{56,1... | collective-permute-start | bytes 98312 | tf_op jit(solution)/shard_map/ppermute | solution.py:15
  157.2 26.8 %all-gather.5.cloned.1.call-done = f32[9,192,256]{1,2,0:T(8,128)} async-done(((f32[9,192,32]{1,2,0:T(8,128)}), f32[9,192,256]{1,2,0:T(8,128)}) %all-gather.5.cloned.1.call-update) | async-done | bytes 1769488 | tf_op jit(solution)/shard_map/all_gather | solution.py:109
  193.4 4.6 %fusion.16 = f32[9,24,256]{2,1,0:T(8,128)S(1)} fusion(f32[9,192,256]{1,2,0:T(8,128)} %all-gather.5.cloned.1.call-done, f32[9,27,24,192]{3,2,1,0:T(8,128)} %gather.7, pred[9,27]{1,0:T(8,128)(4,1)S(1)} %get-tuple-element.16, pred[9,27]{1,0:T(8,128)(4,1)S(1)} %fusion.47), kind=kOutput, calls=%fused_computation.24 | convolution fusion | flops 1148857344 | bytes 6470118 | tf_op jit(solution)/shard_map/ijrc,jcm->irm/dot_general | solution.py:53
  198.1 30.0 %collective-permute-done.7 = f32[9,192,256]{2,1,0:T(8,128)} collective-permute-done((f32[9,192,256]{2,1,0:T(8,128)}, f32[9,192,256]{2,1,0:T(8,128)}, u32[]{:S(2)}, u32[]{:S(2)}) %collective-permute-start.7) | collective-permute-done | bytes 1769504 | tf_op jit(solution)/shard_map/ppermute | solution.py:24
  232.1 4.1 %fusion.40 = f32[9,24,256]{2,1,0:T(8,128)} fusion(f32[9,24,256]{2,1,0:T(8,128)S(1)} %fusion.43, f32[9,192,256]{2,1,0:T(8,128)} %collective-permute-done.8, f32[9,27,24,192]{3,2,1,0:T(8,128)S(1)} %bitcast.126, pred[9,27]{1,0:T(8,128)(4,1)S(1)} %get-tuple-element.16, pred[9,27]{1,0:T(8,128)(4,1)S(1)} %fusion.47), kind=kOutput, calls=%fused_computation.32 | convolution fusion | flops 1148912640 | bytes 6691302 | tf_op jit(solution)/shard_map/ijrc,jcm->irm/dot_general | solution.py:53
  248.4 5.1 %all-to-all-done.1 = f32[8,1,6912]{2,1,0:T(1,128)S(1)} async-done(((f32[8,1,6912]{2,1,0:T(1,128)}), f32[8,1,6912]{2,1,0:T(1,128)S(1)}, u32[]{:S(2)}, u32[]{:S(2)}) %all-to-all-start.1) | async-done | bytes 221216 | tf_op jit(solution)/shard_map/all_to_all | solution.py:61
  263.7 7.3 %convolution_bitcast_fusion = f32[65536]{0:T(1024)S(1)} fusion(f32[1728,128]{0,1:T(8,128)S(1)} %bitcast.139, f32[1728,256]{1,0:T(8,128)} %bitcast.138, f32[1728,256]{1,0:T(8,128)S(1)} %bitcast.129), kind=kOutput, calls=%fused_computation.1 | convolution fusion | flops 1359839232 | bytes 4685824
  271.1 4.3 %collective-permute-start.9 = (f32[65792]{0:T(1024)S(1)}, f32[65792]{0:T(1024)S(1)}, u32[]{:S(2)}, u32[]{:S(2)}) collective-permute-start(f32[65792]{0:T(1024)S(1)} %pad_maximum_fusion.1), channel_id=1, source_target_pairs={{0,8},{8,0},{16,24},{24,16},{32,40},{40,32},{48,56},{56,48},{64,72... | collective-permute-start | bytes 789512 | tf_op jit(solution)/shard_map/ppermute | solution.py:15
  275.4 6.1 %collective-permute-done.9 = f32[65792]{0:T(1024)S(1)} collective-permute-done((f32[65792]{0:T(1024)S(1)}, f32[65792]{0:T(1024)S(1)}, u32[]{:S(2)}, u32[]{:S(2)}) %collective-permute-start.9) | collective-permute-done | bytes 263200 | tf_op jit(solution)/shard_map/ppermute | solution.py:15
  281.6 8.7 %collective-permute-done.10 = f32[65792]{0:T(1024)S(1)} collective-permute-done((f32[65792]{0:T(1024)S(1)}, f32[65792]{0:T(1024)S(1)}, u32[]{:S(2)}, u32[]{:S(2)}) %collective-permute-start.10) | collective-permute-done | bytes 263200 | tf_op jit(solution)/shard_map/ppermute | solution.py:15
  290.5 6.4 %collective-permute-done.11 = f32[65792]{0:T(1024)S(1)} collective-permute-done((f32[65792]{0:T(1024)S(1)}, f32[65792]{0:T(1024)S(1)}, u32[]{:S(2)}, u32[]{:S(2)}) %collective-permute-start.11) | collective-permute-done | bytes 263200 | tf_op jit(solution)/shard_map/ppermute | solution.py:15
  298.0 10.9 %collective-permute-done.12 = f32[65792]{0:T(1024)S(1)} collective-permute-done((f32[65792]{0:T(1024)S(1)}, f32[65792]{0:T(1024)S(1)}, u32[]{:S(2)}, u32[]{:S(2)}) %collective-permute-start.12) | collective-permute-done | bytes 263200 | tf_op jit(solution)/shard_map/ppermute | solution.py:15
  309.6 5.5 %collective-permute-start.13 = (f32[65792]{0:T(1024)}, f32[65792]{0:T(1024)}, u32[]{:S(2)}, u32[]{:S(2)}) collective-permute-start(f32[65792]{0:T(1024)} %add.138), channel_id=1, source_target_pairs={{0,128},{8,136},{16,144},{24,152},{32,160},{40,168},{48,176},{56,1... | collective-permute-start | bytes 789512 | tf_op jit(solution)/shard_map/ppermute | solution.py:15
  316.4 10.9 %collective-permute-done.13 = f32[65792]{0:T(1024)} collective-permute-done((f32[65792]{0:T(1024)}, f32[65792]{0:T(1024)}, u32[]{:S(2)}, u32[]{:S(2)}) %collective-permute-start.13) | collective-permute-done | bytes 263200 | tf_op jit(solution)/shard_map/ppermute | solution.py:15
  (109 shorter events, 96.0 us)
Async XLA Ops:
  7.2 147.5 %copy-start = (f32[9,192,192]{2,1,0:T(8,128)S(1)}, f32[9,192,192]{2,1,0:T(8,128)}, u32[]{:S(2)}) copy-start(f32[9,192,192]{2,1,0:T(8,128)} %param.6) | copy-start | bytes 3981316
  7.2 33.8 %all-gather.3.cloned.1.call-start = ((), (), s32[]{:S(2)}) async-start(), calls=%async_computation.2 | async-start | bytes 2654208 | tf_op jit(solution)/shard_map/all_gather | solution.py:82
  9.3 35.8 %copy-start.10 = (s32[9,27]{1,0:T(8,128)S(1)}, s32[9,27]{1,0:T(8,128)}, u32[]{:S(2)}) copy-start(s32[9,27]{1,0:T(8,128)} %param.7) | copy-start | bytes 2920
  9.3 174.6 %all-gather.5.cloned.1.call-start = ((), (), s32[]{:S(2)}) async-start(), calls=%async_computation.3 | async-start | bytes 2654208 | tf_op jit(solution)/shard_map/all_gather | solution.py:109
  43.0 108.3 %copy-start.2 = (f32[9,192,256]{2,1,0:T(8,128)}, f32[9,192,256]{2,1,0:T(8,128)S(1)}, u32[]{:S(2)}) copy-start(f32[9,192,256]{2,1,0:T(8,128)S(1)} %copy.50) | copy-start | bytes 5308420
  43.0 40.9 %collective-permute-start = (f32[9,192,256]{2,1,0:T(8,128)S(1)}, f32[9,192,256]{2,1,0:T(8,128)}, u32[]{:S(2)}, u32[]{:S(2)}) collective-permute-start(f32[9,192,256]{2,1,0:T(8,128)S(1)} %copy.50), channel_id=1, source_target_pairs={{0,8},{8,16},{16,24},{24,32},{32,40},{40,48},{48,56},{56,64},{64,7... | collective-permute-start | bytes 5308424 | tf_op jit(solution)/shard_map/ppermute | solution.py:24
  44.6 42.8 %collective-permute-start.1 = (f32[9,192,256]{2,1,0:T(8,128)S(1)}, f32[9,192,256]{2,1,0:T(8,128)}, u32[]{:S(2)}, u32[]{:S(2)}) collective-permute-start(f32[9,192,256]{2,1,0:T(8,128)S(1)} %copy.50), channel_id=1, source_target_pairs={{8,0},{16,8},{24,16},{32,24},{40,32},{48,40},{56,48},{64,56},{72,6... | collective-permute-start | bytes 5308424 | tf_op jit(solution)/shard_map/ppermute | solution.py:25
  122.8 6.2 %collective-permute-start.2 = (f32[256,32]{0,1:T(8,128)S(1)}, f32[256,32]{0,1:T(8,128)S(1)}, u32[]{:S(2)}, u32[]{:S(2)}) collective-permute-start(f32[256,32]{0,1:T(8,128)S(1)} %convolution_bitcast_fusion.3), channel_id=1, source_target_pairs={{0,8},{8,0},{16,24},{24,16},{32,40},{40,32},{48,56},{56,48},{64,72... | collective-permute-start | bytes 98312 | tf_op jit(solution)/shard_map/ppermute | solution.py:15
  129.1 5.4 %collective-permute-start.3 = (f32[256,32]{0,1:T(8,128)S(1)}, f32[256,32]{0,1:T(8,128)S(1)}, u32[]{:S(2)}, u32[]{:S(2)}) collective-permute-start(f32[256,32]{0,1:T(8,128)S(1)} %add.128), channel_id=1, source_target_pairs={{0,16},{8,24},{16,0},{24,8},{32,48},{40,56},{48,32},{56,40},{64,80... | collective-permute-start | bytes 98312 | tf_op jit(solution)/shard_map/ppermute | solution.py:15
  134.5 4.1 %collective-permute-start.4 = (f32[256,32]{0,1:T(8,128)S(1)}, f32[256,32]{0,1:T(8,128)S(1)}, u32[]{:S(2)}, u32[]{:S(2)}) collective-permute-start(f32[256,32]{0,1:T(8,128)S(1)} %add.129), channel_id=1, source_target_pairs={{0,32},{8,40},{16,48},{24,56},{32,0},{40,8},{48,16},{56,24},{64,96... | collective-permute-start | bytes 98312 | tf_op jit(solution)/shard_map/ppermute | solution.py:15
  138.6 4.8 %collective-permute-start.5 = (f32[256,32]{0,1:T(8,128)S(1)}, f32[256,32]{0,1:T(8,128)S(1)}, u32[]{:S(2)}, u32[]{:S(2)}) collective-permute-start(f32[256,32]{0,1:T(8,128)S(1)} %add.130), channel_id=1, source_target_pairs={{0,64},{8,72},{16,80},{24,88},{32,96},{40,104},{48,112},{56,120},{... | collective-permute-start | bytes 98312 | tf_op jit(solution)/shard_map/ppermute | solution.py:15
  143.4 7.8 %collective-permute-start.6 = (f32[256,32]{0,1:T(8,128)S(1)}, f32[256,32]{0,1:T(8,128)S(1)}, u32[]{:S(2)}, u32[]{:S(2)}) collective-permute-start(f32[256,32]{0,1:T(8,128)S(1)} %add.131), channel_id=1, source_target_pairs={{0,128},{8,136},{16,144},{24,152},{32,160},{40,168},{48,176},{56,1... | collective-permute-start | bytes 98312 | tf_op jit(solution)/shard_map/ppermute | solution.py:15
  187.0 41.1 %collective-permute-start.7 = (f32[9,192,256]{2,1,0:T(8,128)}, f32[9,192,256]{2,1,0:T(8,128)}, u32[]{:S(2)}, u32[]{:S(2)}) collective-permute-start(f32[9,192,256]{2,1,0:T(8,128)} %copy.57), channel_id=1, source_target_pairs={{0,8},{8,16},{16,24},{24,32},{32,40},{40,48},{48,56},{56,64},{64,7... | collective-permute-start | bytes 5308424 | tf_op jit(solution)/shard_map/ppermute | solution.py:24
  188.4 43.6 %collective-permute-start.8 = (f32[9,192,256]{2,1,0:T(8,128)}, f32[9,192,256]{2,1,0:T(8,128)}, u32[]{:S(2)}, u32[]{:S(2)}) collective-permute-start(f32[9,192,256]{2,1,0:T(8,128)} %copy.57), channel_id=1, source_target_pairs={{8,0},{16,8},{24,16},{32,24},{40,32},{48,40},{56,48},{64,56},{72,6... | collective-permute-start | bytes 5308424 | tf_op jit(solution)/shard_map/ppermute | solution.py:25
  191.4 40.7 %slice-start = ((s8[5971968]{0:T(1024)(128)(4,1)}), s8[1777664]{0:T(1024)(128)(4,1)S(1)}, s32[]{:S(2)}) async-start(s8[5971968]{0:T(1024)(128)(4,1)} %bitcast.125), calls=%async_computation.4 | async-start | bytes 3555328
  193.4 38.7 %slice-start.1 = ((s8[5971968]{0:T(1024)(128)(4,1)}), s8[4194304]{0:T(1024)(128)(4,1)S(1)}, s32[]{:S(2)}) async-start(s8[5971968]{0:T(1024)(128)(4,1)} %bitcast.125), calls=%async_computation.5 | async-start | bytes 8388608
  242.7 10.8 %all-to-all-start.1 = ((f32[8,1,6912]{2,1,0:T(1,128)}), f32[8,1,6912]{2,1,0:T(1,128)S(1)}, u32[]{:S(2)}, u32[]{:S(2)}) async-start(f32[8,1,6912]{2,1,0:T(1,128)} %reshape.135), calls=%async_computation.1 | async-start | bytes 442368 | tf_op jit(solution)/shard_map/all_to_all | solution.py:61
  271.0 44.2 %copy-start.6 = (f32[9,192,32]{1,0,2:T(8,128)S(1)}, f32[9,192,32]{1,0,2:T(8,128)}, u32[]{:S(2)}) copy-start(f32[9,192,32]{1,0,2:T(8,128)} %copy.56) | copy-start | bytes 663556
  271.0 45.0 %copy-start.5 = (f32[9,24,8,32]{1,2,0,3:T(8,128)S(1)}, f32[9,24,8,32]{1,2,0,3:T(8,128)}, u32[]{:S(2)}) copy-start(f32[9,24,8,32]{1,2,0,3:T(8,128)} %copy.76) | copy-start | bytes 663556
  271.1 10.4 %collective-permute-start.9 = (f32[65792]{0:T(1024)S(1)}, f32[65792]{0:T(1024)S(1)}, u32[]{:S(2)}, u32[]{:S(2)}) collective-permute-start(f32[65792]{0:T(1024)S(1)} %pad_maximum_fusion.1), channel_id=1, source_target_pairs={{0,8},{8,0},{16,24},{24,16},{32,40},{40,32},{48,56},{56,48},{64,72... | collective-permute-start | bytes 789512 | tf_op jit(solution)/shard_map/ppermute | solution.py:15
  281.5 8.8 %collective-permute-start.10 = (f32[65792]{0:T(1024)S(1)}, f32[65792]{0:T(1024)S(1)}, u32[]{:S(2)}, u32[]{:S(2)}) collective-permute-start(f32[65792]{0:T(1024)S(1)} %fusion.73), channel_id=1, source_target_pairs={{0,16},{8,24},{16,0},{24,8},{32,48},{40,56},{48,32},{56,40},{64,80... | collective-permute-start | bytes 789512 | tf_op jit(solution)/shard_map/ppermute | solution.py:15
  290.4 6.5 %collective-permute-start.11 = (f32[65792]{0:T(1024)S(1)}, f32[65792]{0:T(1024)S(1)}, u32[]{:S(2)}, u32[]{:S(2)}) collective-permute-start(f32[65792]{0:T(1024)S(1)} %add.136), channel_id=1, source_target_pairs={{0,32},{8,40},{16,48},{24,56},{32,0},{40,8},{48,16},{56,24},{64,96... | collective-permute-start | bytes 789512 | tf_op jit(solution)/shard_map/ppermute | solution.py:15
  296.9 11.9 %collective-permute-start.12 = (f32[65792]{0:T(1024)S(1)}, f32[65792]{0:T(1024)S(1)}, u32[]{:S(2)}, u32[]{:S(2)}) collective-permute-start(f32[65792]{0:T(1024)S(1)} %add.137), channel_id=1, source_target_pairs={{0,64},{8,72},{16,80},{24,88},{32,96},{40,104},{48,112},{56,120},{... | collective-permute-start | bytes 789512 | tf_op jit(solution)/shard_map/ppermute | solution.py:15
  309.6 17.6 %collective-permute-start.13 = (f32[65792]{0:T(1024)}, f32[65792]{0:T(1024)}, u32[]{:S(2)}, u32[]{:S(2)}) collective-permute-start(f32[65792]{0:T(1024)} %add.138), channel_id=1, source_target_pairs={{0,128},{8,136},{16,144},{24,152},{32,160},{40,168},{48,176},{56,1... | collective-permute-start | bytes 789512 | tf_op jit(solution)/shard_map/ppermute | solution.py:15
  (6 other events, 118.8 us)
Sparse Core Ops, SparseCore 0:
  9.8 31.0 all-gather.2
  157.3 26.6 all-gather.4

commit v2 on v1

--- a/solution.py
+++ b/solution.py
@@ -21,8 +21,23 @@
     count = lax.axis_size("space")
     forward = [(i, (i + 1) % count) for i in range(count)]
     backward = [((i + 1) % count, i) for i in range(count)]
-    low = lax.ppermute(block[block.shape[0] - width :], "space", forward)
-    high = lax.ppermute(block[:width], "space", backward)
+    mode_count = lax.axis_size("mode")
+    core = lax.axis_index("mode") % 2
+    half = block.shape[2] // 2
+    siblings = [(i, i ^ 1) for i in range(mode_count)]
+
+    def send(piece, pairs):
+        mine = lax.dynamic_slice_in_dim(piece, core * half, half, axis=2)
+        got = lax.ppermute(mine, "space", pairs)
+        other = lax.ppermute(got, "mode", siblings)
+        return jnp.where(
+            core == 0,
+            jnp.concatenate([got, other], axis=2),
+            jnp.concatenate([other, got], axis=2),
+        )
+
+    low = send(block[block.shape[0] - width :], forward)
+    high = send(block[:width], backward)
     return low, high
 
 
@@ -30,19 +45,26 @@
     block_rows, neigh = local_ids.shape
     columns = jnp.arange(ext_blocks, dtype=jnp.int32)
     onehot = local_ids[:, :, None] == columns[None, None, :]
-    offsets = jnp.arange(neigh, dtype=jnp.int32)
-    which = jnp.sum(jnp.where(onehot, offsets[None, :, None], 0), axis=1)
-    valid = jnp.any(onehot, axis=1)
-    flat = (jnp.arange(block_rows, dtype=jnp.int32)[:, None] * neigh + which).reshape(-1)
     rows, cols = force_blocks.shape[2], force_blocks.shape[3]
-    table = force_blocks.reshape(block_rows * neigh, rows * cols)
-    picked = jnp.take(table, flat, axis=0).reshape(block_rows, ext_blocks, rows, cols)
-    return jnp.where(valid[:, :, None, None], picked, 0.0)
+    table = force_blocks.reshape(block_rows, neigh, rows * cols)
+    picked = jnp.einsum(
+        "ikj,ikx->ijx",
+        onehot.astype(jnp.float32),
+        table,
+        precision=HIGHEST,
+        preferred_element_type=jnp.float32,
+    )
+    return picked.reshape(block_rows, ext_blocks, rows, cols)
 
 
 def apply_dense(dense, low, own, high):
     width = low.shape[0]
     own_count = own.shape[0]
+    mode_count = lax.axis_size("mode")
+
+    def split(field):
+        return field.reshape(field.shape[0], field.shape[1], mode_count, -1)
+
     parts = (
         (dense[:, width : width + own_count], own),
         (dense[:, :width], low),
@@ -51,15 +73,16 @@
     total = None
     for coeffs, field in parts:
         product = jnp.einsum(
-            "ijrc,jcm->irm",
+            "ijrc,jcdm->dirm",
             coeffs,
-            field,
+            split(field),
             precision=HIGHEST,
             preferred_element_type=jnp.float32,
         )
         total = product if total is None else total + product
-    regrouped = lax.all_to_all(total, "mode", split_axis=2, concat_axis=1, tiled=True)
-    return regrouped.reshape(-1, regrouped.shape[2])
+    regrouped = lax.all_to_all(total, "mode", split_axis=0, concat_axis=0, tiled=True)
+    regrouped = jnp.transpose(regrouped, (1, 0, 2, 3))
+    return regrouped.reshape(-1, regrouped.shape[3])
 
 
 def local(vectors, force_blocks, inverse_blocks, neighbours):
@@ -107,31 +130,58 @@
         preferred_element_type=jnp.float32,
     )
     full_s = lax.all_gather(search_raw, "mode", axis=2, tiled=True)
+    flat_s = full_s.reshape(row_count, mode_count)
+    own_s = search_raw.reshape(row_count, col_count)
+
+    squares = jnp.sum(flat_s * flat_s, axis=0)
+    cross = jnp.einsum(
+        "ra,rgj->agj",
+        flat_s,
+        jnp.stack([vectors, own_s, image_x], axis=1),
+        precision=HIGHEST,
+        preferred_element_type=jnp.float32,
+    )
+    x_s = jnp.einsum(
+        "ra,rgj->agj",
+        flat_x,
+        jnp.stack([vectors, own_s], axis=1),
+        precision=HIGHEST,
+        preferred_element_type=jnp.float32,
+    )
+    packed = jnp.concatenate([cross.reshape(-1), x_s.reshape(-1), squares])
+    summed = space_sum(packed)
+    cross_sum = summed[: cross.size].reshape(cross.shape)
+    x_s_sum = summed[cross.size : cross.size + x_s.size].reshape(x_s.shape)
+    scales_all = lax.rsqrt(summed[cross.size + x_s.size :] / total_rows + 1e-06)
+    scales_own = lax.dynamic_slice_in_dim(scales_all, mode_index * col_count, col_count)
+
     low_s, high_s = halo(full_s, CELLS)
     image_s = apply_dense(dense, low_s, full_s, high_s)
-    flat_s = full_s.reshape(row_count, mode_count)
-    own_s = search_raw.reshape(row_count, col_count)
-
-    squares = jnp.sum(flat_s * flat_s, axis=0)
     basis = jnp.concatenate([flat_x, flat_s], axis=1)
-    columns = jnp.stack([vectors, own_s, image_x, image_s], axis=1)
-    gram_part = jnp.einsum(
-        "ra,rgj->agj", basis, columns, precision=HIGHEST, preferred_element_type=jnp.float32
-    )
-    packed = jnp.concatenate([gram_part.reshape(-1), squares])
-    summed = space_sum(packed)
-    gram_sum = summed[: gram_part.size].reshape(gram_part.shape)
-    scales_all = lax.rsqrt(summed[gram_part.size :] / total_rows + 1e-06)
-    scales_own = lax.dynamic_slice_in_dim(scales_all, mode_index * col_count, col_count)
+    last = space_sum(
+        jnp.einsum(
+            "ra,rj->aj", basis, image_s, precision=HIGHEST, preferred_element_type=jnp.float32
+        )
+    )
 
     w_block = own_s * scales_own
     hw_block = image_s * scales_own
-    row_scale = jnp.concatenate([jnp.ones((mode_count,), jnp.float32), scales_all])
-    ones_own = jnp.ones((col_count,), jnp.float32)
-    col_scale = jnp.stack([ones_own, scales_own, ones_own, scales_own])
-    gram = gram_sum * row_scale[:, None, None] * col_scale[None] / total_rows
-    gram_b = gram[:, 0:2]
-    gram_a = gram[:, 2:4]
+    col = scales_own[None, :]
+    row = scales_all[:, None]
+    gram_b = jnp.concatenate(
+        [
+            jnp.stack([x_s_sum[:, 0], x_s_sum[:, 1] * col], axis=1) / total_rows,
+            jnp.stack([cross_sum[:, 0] * row, cross_sum[:, 1] * row * col], axis=1) / total_rows,
+        ],
+        axis=0,
+    )
+    gram_a = jnp.concatenate(
+        [
+            jnp.stack([rayleigh, last[:mode_count] * col / total_rows], axis=1),
+            jnp.stack([cross_sum[:, 2] * row, last[mode_count:] * row * col], axis=1) / total_rows,
+        ],
+        axis=0,
+    )
     return (w_block, hw_block, gram_a, gram_b)
 
 

time: 347 us -> 381 us (1.098)
  matrix products: 39.1 us -> 82.6 us
  waiting for transfers between devices: 165 us -> 139 us
  starting transfers between devices: 30.4 us -> 47.9 us
  blocking collectives: 11.1 us -> 0 us
  local copies, waits for them, and re-layouts: 68.1 us -> 75.9 us
    dot_general x6 -> x9, matrix products: 25.1 us -> 71.6 us  [the longest x6 59.3 us: apply_dense(): jnp.einsum('ijrc,jcdm->dirm', coeffs, split(field), precision=HIGHEST, pr...]
    ppermute x0 -> x8, local copies, waits for them, and re-layouts: none -> 18.5 us  [the longest x4 10.4 us: send(): other = lax.ppermute(got, 'mode', siblings)]
    ppermute x10 -> x15, waiting for transfers between devices: 60.5 us -> 45.5 us  [space_sum(): value = value + lax.ppermute(value, 'space', pairs)]
    gather x2 -> x0, local copies, waits for them, and re-layouts: 14.9 us -> none  [dense_rows(): jnp.take(table, flat, axis=0).reshape(block_rows, ext_blocks, rows, cols)]
    ppermute x10 -> x15, starting transfers between devices: 22 us -> 35.6 us  [space_sum(): value = value + lax.ppermute(value, 'space', pairs)]
    reshape x3 -> x7, local copies, waits for them, and re-layouts: 9.42 us -> 20.6 us  [the longest x1 7.34 us: dense_rows(): table = force_blocks.reshape(block_rows, neigh, rows * cols)]
    all_to_all x1 -> x0, blocking collectives: 11.1 us -> none  [apply_dense(): lax.all_to_all(total, 'mode', split_axis=2, concat_axis=1, tiled=True)]
    ppermute x4 -> x8, waiting for transfers between devices: 40.7 us -> 29.7 us  [the longest x4 29.7 us: send(): got = lax.ppermute(mine, 'space', pairs)]
  transfers between devices with their start and end apart: 17 -> 27, of which waited for: 15 -> 20; matrix products, arithmetic and copies ran while one was open for 14% -> 26% of each run, Pallas kernels for 0% -> 0%
where the time goes in v2:
time: 381 us; the launch traced here: 375 us
  waiting for transfers between devices  139 us (36%)
  matrix products  82.6 us (22%)
  local copies, waits for them, and re-layouts  75.9 us (20%)
  starting transfers between devices  47.9 us (13%)
  between operations  14.9 us (4%)
  other arithmetic  14.3 us (4%)
    dot_general x6, matrix products, apply_dense(): jnp.einsum('ijrc,jcdm->dirm', coeffs, split(field), precision=HIGHEST, pr...  59.3 us
    ppermute x15, waiting for transfers between devices, space_sum(): value = value + lax.ppermute(value, 'space', pairs)  45.5 us
    ppermute x15, starting transfers between devices, space_sum(): value = value + lax.ppermute(value, 'space', pairs)  35.6 us
    all_gather x1, waiting for transfers between devices, local(): full_x = lax.all_gather(stacked_x, 'mode', axis=2, tiled=True)  31.6 us
    ppermute x4, waiting for transfers between devices, send(): got = lax.ppermute(mine, 'space', pairs)  29.7 us
    all_gather x1, waiting for transfers between devices, local(): full_s = lax.all_gather(search_raw, 'mode', axis=2, tiled=True)  22 us
    unnamed x43, local copies, waits for them, and re-layouts  11.1 us
    all_to_all x2, waiting for transfers between devices, apply_dense(): lax.all_to_all(total, 'mode', split_axis=0, concat_axis=0, tiled=True)  10.5 us
  transfers between devices with their start and end apart: 27, of which 20 were waited for; matrix products, arithmetic and copies ran while one was open for 26% of the time, Pallas kernels for 0%

profile of v2, /device:TPU:2, one launch (start us, length us, event | category | flops | bytes accessed | tf_op | source)
XLA Modules:
  0.0 375.0 jit_solution(15624094461837809021)
XLA Ops:
  9.4 31.6 %all-gather.3.cloned.1.call-done = f32[9,192,256]{1,2,0:T(8,128)} async-done(((f32[9,192,32]{1,2,0:T(8,128)}), f32[9,192,256]{1,2,0:T(8,128)}) %all-gather.3.cloned.1.call-update) | async-done | bytes 1769488 | tf_op jit(solution)/shard_map/all_gather | solution.py:105
  45.7 7.3 %reshape.103 = f32[9,27,4608]{2,1,0:T(8,128)} reshape(f32[9,27,24,192]{3,2,1,0:T(8,128)} %param.5) | data formatting | bytes 8957952 | tf_op jit(solution)/shard_map/reshape | solution.py:49
  53.1 12.7 %collective-permute-done = f32[9,192,128]{2,1,0:T(8,128)} collective-permute-done((f32[9,192,128]{2,1,0:T(8,128)}, f32[9,192,128]{2,1,0:T(8,128)}, u32[]{:S(2)}, u32[]{:S(2)}) %collective-permute-start) | collective-permute-done | bytes 884768 | tf_op jit(solution)/shard_map/ppermute | solution.py:31
  67.1 7.5 %fusion.93 = f32[9,27,4608]{2,1,0:T(8,128)} fusion(f32[9,27,4608]{2,1,0:T(8,128)} %reshape.103, s32[9,27]{1,0:T(8,128)S(1)} %fusion.104), kind=kOutput, calls=%fused_computation.61 | convolution fusion | flops 362803616 | bytes 8958924 | tf_op jit(solution)/shard_map/ikj,ikx->ijx/dot_general | solution.py:50
  74.7 6.8 %reshape.104 = f32[9,27,24,192]{3,2,1,0:T(8,128)} reshape(f32[9,27,4608]{2,1,0:T(8,128)} %fusion.93) | data formatting | bytes 8957952 | tf_op jit(solution)/shard_map/reshape | solution.py:57
  81.5 9.7 %fusion.34 = f32[8,9,24,32]{3,2,0,1:T(8,128)} fusion(f32[9,192,8,32]{1,3,2,0:T(8,128)} %bitcast.181, f32[9,27,24,192]{3,2,1,0:T(8,128)} %reshape.104), kind=kOutput, calls=%fused_computation.40 | convolution fusion | flops 1146617856 | bytes 4571136 | tf_op jit(solution)/shard_map/ijrc,jcdm->dirm/dot_general | solution.py:75
  97.9 10.7 %fusion.84 = f32[8,9,24,32]{3,2,0,1:T(8,128)} fusion(f32[8,9,24,32]{3,2,0,1:T(8,128)} %fusion.34, f32[9,27,24,192]{3,2,1,0:T(8,128)} %reshape.104, f32[9,192,4,32]{1,3,2,0:T(8,128)} %bitcast.192, f32[9,192,4,32]{1,3,2,0:T(8,128)} %bitcast.189, pred[]{:T(512)S(6)} %eq.28), kind=kOutput, calls=%fused_computation.50 | convolution fusion | flops 1148000256 | bytes 5455873 | tf_op jit(solution)/shard_map/ijrc,jcdm->dirm/dot_general | solution.py:75
  111.2 8.8 %fusion.79 = f32[8,9,24,32]{3,2,0,1:T(8,128)S(1)} fusion(f32[8,9,24,32]{3,2,0,1:T(8,128)} %fusion.84, f32[9,27,24,192]{3,2,1,0:T(8,128)} %reshape.104, f32[9,192,4,32]{1,3,2,0:T(8,128)} %bitcast.193, f32[9,192,4,32]{1,3,2,0:T(8,128)S(1)} %bitcast.188, pred[]{:T(512)S(6)} %eq.28), kind=kOutput, calls=%fused_computation.49 | convolution fusion | flops 1148000256 | bytes 5160961 | tf_op jit(solution)/shard_map/ijrc,jcdm->dirm/dot_general | solution.py:75
  121.2 4.0 %all-to-all-start = ((f32[8,1,6912]{2,1,0:T(1,128)}), f32[8,1,6912]{2,1,0:T(1,128)}, u32[]{:S(2)}, u32[]{:S(2)}) async-start(f32[8,1,6912]{2,1,0:T(1,128)} %reshape.135), calls=%async_computation | async-start | bytes 442368 | tf_op jit(solution)/shard_map/all_to_all | solution.py:83
  127.7 4.6 %all-to-all-done = f32[8,1,6912]{2,1,0:T(1,128)} async-done(((f32[8,1,6912]{2,1,0:T(1,128)}), f32[8,1,6912]{2,1,0:T(1,128)}, u32[]{:S(2)}, u32[]{:S(2)}) %all-to-all-start) | async-done | bytes 221216 | tf_op jit(solution)/shard_map/all_to_all | solution.py:83
  159.6 3.9 %collective-permute-start.7 = (f32[256,32]{0,1:T(8,128)S(1)}, f32[256,32]{0,1:T(8,128)S(1)}, u32[]{:S(2)}, u32[]{:S(2)}) collective-permute-start(f32[256,32]{0,1:T(8,128)S(1)} %add.109), channel_id=1, source_target_pairs={{0,64},{8,72},{16,80},{24,88},{32,96},{40,104},{48,112},{56,120},{... | collective-permute-start | bytes 98312 | tf_op jit(solution)/shard_map/ppermute | solution.py:15
  165.4 4.6 %collective-permute-start.8 = (f32[256,32]{0,1:T(8,128)S(1)}, f32[256,32]{0,1:T(8,128)S(1)}, u32[]{:S(2)}, u32[]{:S(2)}) collective-permute-start(f32[256,32]{0,1:T(8,128)S(1)} %add.110), channel_id=1, source_target_pairs={{0,128},{8,136},{16,144},{24,152},{32,160},{40,168},{48,176},{56,1... | collective-permute-start | bytes 98312 | tf_op jit(solution)/shard_map/ppermute | solution.py:15
  187.5 22.0 %all-gather.5.cloned.1.call-done = f32[9,192,256]{1,2,0:T(8,128)} async-done(((f32[9,192,32]{1,2,0:T(8,128)}), f32[9,192,256]{1,2,0:T(8,128)}) %all-gather.5.cloned.1.call-update) | async-done | bytes 1769488 | tf_op jit(solution)/shard_map/all_gather | solution.py:132
  233.2 15.8 %collective-permute-done.14 = f32[9,192,128]{2,1,0:T(8,128)} collective-permute-done((f32[9,192,128]{2,1,0:T(8,128)}, f32[9,192,128]{2,1,0:T(8,128)}, u32[]{:S(2)}, u32[]{:S(2)}) %collective-permute-start.14) | collective-permute-done | bytes 884768 | tf_op jit(solution)/shard_map/ppermute | solution.py:31
  254.4 4.0 %collective-permute-done.11 = f32[41216]{0:T(1024)S(1)} collective-permute-done((f32[41216]{0:T(1024)S(1)}, f32[41216]{0:T(1024)S(1)}, u32[]{:S(2)}, u32[]{:S(2)}) %collective-permute-start.11) | collective-permute-done | bytes 164896 | tf_op jit(solution)/shard_map/ppermute | solution.py:15
  263.7 4.4 %collective-permute-done.12 = f32[41216]{0:T(1024)S(1)} collective-permute-done((f32[41216]{0:T(1024)S(1)}, f32[41216]{0:T(1024)S(1)}, u32[]{:S(2)}, u32[]{:S(2)}) %collective-permute-start.12) | collective-permute-done | bytes 164896 | tf_op jit(solution)/shard_map/ppermute | solution.py:15
  268.1 5.7 %collective-permute-start.13 = (f32[41216]{0:T(1024)S(1)}, f32[41216]{0:T(1024)S(1)}, u32[]{:S(2)}, u32[]{:S(2)}) collective-permute-start(f32[41216]{0:T(1024)S(1)} %add.115), channel_id=1, source_target_pairs={{0,128},{8,136},{16,144},{24,152},{32,160},{40,168},{48,176},{56,1... | collective-permute-start | bytes 494600 | tf_op jit(solution)/shard_map/ppermute | solution.py:15
  273.7 9.5 %fusion.49 = f32[8,32,9,24]{1,3,2,0:T(8,128)} fusion(f32[9,27,24,192]{3,2,1,0:T(8,128)} %reshape.104, f32[9,192,8,32,1]{1,3,2,0,4:T(8,128)} %bitcast.180), kind=kOutput, calls=%fused_computation.43 | convolution fusion | flops 1146617856 | bytes 4571136 | tf_op jit(solution)/shard_map/ijrc,jcdm->dirm/dot_general | solution.py:75
  292.0 10.8 %fusion.74 = f32[8,32,9,24]{1,3,2,0:T(8,128)} fusion(f32[8,32,9,24]{1,3,2,0:T(8,128)} %fusion.49, f32[9,27,24,192]{3,2,1,0:T(8,128)} %reshape.104, f32[9,192,4,32]{1,3,2,0:T(8,128)} %bitcast.194, f32[9,192,4,32]{1,3,2,0:T(8,128)} %bitcast.190, pred[]{:T(512)S(6)} %eq.28), kind=kOutput, calls=%fused_computation.48 | convolution fusion | flops 1148000256 | bytes 5455873 | tf_op jit(solution)/shard_map/ijrc,jcdm->dirm/dot_general | solution.py:75
  305.3 9.8 %fusion.69 = f32[8,9,24,32]{3,2,1,0:T(8,128)} fusion(f32[8,32,9,24]{1,3,2,0:T(8,128)} %fusion.74, f32[9,27,24,192]{3,2,1,0:T(8,128)} %reshape.104, f32[9,192,4,32]{1,3,2,0:T(8,128)} %bitcast.191, f32[9,192,4,32]{1,3,2,0:T(8,128)S(1)} %bitcast.187, pred[]{:T(512)S(6)} %eq.28), kind=kOutput, calls=%fused_computation.47 | convolution fusion | flops 1148000256 | bytes 5160961 | tf_op jit(solution)/shard_map/ijrc,jcdm->dirm/dot_general | solution.py:75
  322.3 6.0 %all-to-all-done.1 = f32[8,1,6912]{2,1,0:T(1,128)S(1)} async-done(((f32[8,1,6912]{2,1,0:T(1,128)}), f32[8,1,6912]{2,1,0:T(1,128)S(1)}, u32[]{:S(2)}, u32[]{:S(2)}) %all-to-all-start.1) | async-done | bytes 221216 | tf_op jit(solution)/shard_map/all_to_all | solution.py:83
  348.3 4.1 %collective-permute-done.20 = f32[512,32]{0,1:T(8,128)S(1)} collective-permute-done((f32[512,32]{0,1:T(8,128)S(1)}, f32[512,32]{0,1:T(8,128)S(1)}, u32[]{:S(2)}, u32[]{:S(2)}) %collective-permute-start.20) | collective-permute-done | bytes 65568 | tf_op jit(solution)/shard_map/ppermute | solution.py:15
  352.6 5.4 %collective-permute-done.21 = f32[512,32]{0,1:T(8,128)S(1)} collective-permute-done((f32[512,32]{0,1:T(8,128)S(1)}, f32[512,32]{0,1:T(8,128)S(1)}, u32[]{:S(2)}, u32[]{:S(2)}) %collective-permute-start.21) | collective-permute-done | bytes 65568 | tf_op jit(solution)/shard_map/ppermute | solution.py:15
  360.6 5.6 %collective-permute-done.22 = f32[512,32]{0,1:T(8,128)S(1)} collective-permute-done((f32[512,32]{0,1:T(8,128)S(1)}, f32[512,32]{0,1:T(8,128)S(1)}, u32[]{:S(2)}, u32[]{:S(2)}) %collective-permute-start.22) | collective-permute-done | bytes 65568 | tf_op jit(solution)/shard_map/ppermute | solution.py:15
  (157 shorter events, 144.6 us)
Async XLA Ops:
  7.2 33.8 %all-gather.3.cloned.1.call-start = ((), (), s32[]{:S(2)}) async-start(), calls=%async_computation.2 | async-start | bytes 2654208 | tf_op jit(solution)/shard_map/all_gather | solution.py:105
  43.7 22.1 %collective-permute-start = (f32[9,192,128]{2,1,0:T(8,128)}, f32[9,192,128]{2,1,0:T(8,128)}, u32[]{:S(2)}, u32[]{:S(2)}) collective-permute-start(f32[9,192,128]{2,1,0:T(8,128)} %copy.88), channel_id=1, source_target_pairs={{0,8},{8,16},{16,24},{24,32},{32,40},{40,48},{48,56},{56,64},{64,7... | collective-permute-start | bytes 2654216 | tf_op jit(solution)/shard_map/ppermute | solution.py:31
  45.1 21.8 %collective-permute-start.2 = (f32[9,192,128]{2,1,0:T(8,128)}, f32[9,192,128]{2,1,0:T(8,128)}, u32[]{:S(2)}, u32[]{:S(2)}) collective-permute-start(f32[9,192,128]{2,1,0:T(8,128)} %copy.88), channel_id=1, source_target_pairs={{8,0},{16,8},{24,16},{32,24},{40,32},{48,40},{56,48},{64,56},{72,6... | collective-permute-start | bytes 2654216 | tf_op jit(solution)/shard_map/ppermute | solution.py:31
  65.8 29.5 %collective-permute-start.1 = (f32[9,192,128]{2,1,0:T(8,128)}, f32[9,192,128]{2,1,0:T(8,128)}, u32[]{:S(2)}, u32[]{:S(2)}) collective-permute-start(f32[9,192,128]{2,1,0:T(8,128)} %collective-permute-done), channel_id=1, source_target_pairs={{0,1},{1,0},{2,3},{3,2},{4,5},{5,4},{6,7},{7,6},{8,9},{9,8},{10,11... | collective-permute-start | bytes 2654216 | tf_op jit(solution)/shard_map/ppermute | solution.py:32
  67.0 41.7 %collective-permute-start.3 = (f32[9,192,128]{2,1,0:T(8,128)}, f32[9,192,128]{2,1,0:T(8,128)}, u32[]{:S(2)}, u32[]{:S(2)}) collective-permute-start(f32[9,192,128]{2,1,0:T(8,128)} %collective-permute-done.2), channel_id=1, source_target_pairs={{0,1},{1,0},{2,3},{3,2},{4,5},{5,4},{6,7},{7,6},{8,9},{9,8},{10,11... | collective-permute-start | bytes 2654216 | tf_op jit(solution)/shard_map/ppermute | solution.py:32
  121.2 11.1 %all-to-all-start = ((f32[8,1,6912]{2,1,0:T(1,128)}), f32[8,1,6912]{2,1,0:T(1,128)}, u32[]{:S(2)}, u32[]{:S(2)}) async-start(f32[8,1,6912]{2,1,0:T(1,128)} %reshape.135), calls=%async_computation | async-start | bytes 442368 | tf_op jit(solution)/shard_map/all_to_all | solution.py:83
  125.2 84.3 %all-gather.5.cloned.1.call-start = ((), (), s32[]{:S(2)}) async-start(), calls=%async_computation.3 | async-start | bytes 2654208 | tf_op jit(solution)/shard_map/all_gather | solution.py:132
  144.7 5.5 %collective-permute-start.4 = (f32[256,32]{0,1:T(8,128)S(1)}, f32[256,32]{0,1:T(8,128)S(1)}, u32[]{:S(2)}, u32[]{:S(2)}) collective-permute-start(f32[256,32]{0,1:T(8,128)S(1)} %convolution_bitcast_fusion.3), channel_id=1, source_target_pairs={{0,8},{8,0},{16,24},{24,16},{32,40},{40,32},{48,56},{56,48},{64,72... | collective-permute-start | bytes 98312 | tf_op jit(solution)/shard_map/ppermute | solution.py:15
  150.2 5.4 %collective-permute-start.5 = (f32[256,32]{0,1:T(8,128)S(1)}, f32[256,32]{0,1:T(8,128)S(1)}, u32[]{:S(2)}, u32[]{:S(2)}) collective-permute-start(f32[256,32]{0,1:T(8,128)S(1)} %add.107), channel_id=1, source_target_pairs={{0,16},{8,24},{16,0},{24,8},{32,48},{40,56},{48,32},{56,40},{64,80... | collective-permute-start | bytes 98312 | tf_op jit(solution)/shard_map/ppermute | solution.py:15
  159.6 5.8 %collective-permute-start.7 = (f32[256,32]{0,1:T(8,128)S(1)}, f32[256,32]{0,1:T(8,128)S(1)}, u32[]{:S(2)}, u32[]{:S(2)}) collective-permute-start(f32[256,32]{0,1:T(8,128)S(1)} %add.109), channel_id=1, source_target_pairs={{0,64},{8,72},{16,80},{24,88},{32,96},{40,104},{48,112},{56,120},{... | collective-permute-start | bytes 98312 | tf_op jit(solution)/shard_map/ppermute | solution.py:15
  165.4 7.9 %collective-permute-start.8 = (f32[256,32]{0,1:T(8,128)S(1)}, f32[256,32]{0,1:T(8,128)S(1)}, u32[]{:S(2)}, u32[]{:S(2)}) collective-permute-start(f32[256,32]{0,1:T(8,128)S(1)} %add.110), channel_id=1, source_target_pairs={{0,128},{8,136},{16,144},{24,152},{32,160},{40,168},{48,176},{56,1... | collective-permute-start | bytes 98312 | tf_op jit(solution)/shard_map/ppermute | solution.py:15
  222.6 7.5 %collective-permute-start.9 = (f32[41216]{0:T(1024)}, f32[41216]{0:T(1024)}, u32[]{:S(2)}, u32[]{:S(2)}) collective-permute-start(f32[41216]{0:T(1024)} %pad_maximum_fusion.1), channel_id=1, source_target_pairs={{0,8},{8,0},{16,24},{24,16},{32,40},{40,32},{48,56},{56,48},{64,72... | collective-permute-start | bytes 494600 | tf_op jit(solution)/shard_map/ppermute | solution.py:15
  224.5 24.5 %collective-permute-start.14 = (f32[9,192,128]{2,1,0:T(8,128)}, f32[9,192,128]{2,1,0:T(8,128)}, u32[]{:S(2)}, u32[]{:S(2)}) collective-permute-start(f32[9,192,128]{2,1,0:T(8,128)} %copy.107), channel_id=1, source_target_pairs={{0,8},{8,16},{16,24},{24,32},{32,40},{40,48},{48,56},{56,64},{64,7... | collective-permute-start | bytes 2654216 | tf_op jit(solution)/shard_map/ppermute | solution.py:31
  226.6 34.8 %collective-permute-start.16 = (f32[9,192,128]{2,1,0:T(8,128)}, f32[9,192,128]{2,1,0:T(8,128)}, u32[]{:S(2)}, u32[]{:S(2)}) collective-permute-start(f32[9,192,128]{2,1,0:T(8,128)} %copy.107), channel_id=1, source_target_pairs={{8,0},{16,8},{24,16},{32,24},{40,32},{48,40},{56,48},{64,56},{72,6... | collective-permute-start | bytes 2654216 | tf_op jit(solution)/shard_map/ppermute | solution.py:31
  231.1 21.6 %collective-permute-start.10 = (f32[41216]{0:T(1024)S(1)}, f32[41216]{0:T(1024)S(1)}, u32[]{:S(2)}, u32[]{:S(2)}) collective-permute-start(f32[41216]{0:T(1024)S(1)} %fusion.111), channel_id=1, source_target_pairs={{0,16},{8,24},{16,0},{24,8},{32,48},{40,56},{48,32},{56,40},{64,80... | collective-permute-start | bytes 494600 | tf_op jit(solution)/shard_map/ppermute | solution.py:15
  249.0 40.3 %collective-permute-start.15 = (f32[9,192,128]{2,1,0:T(8,128)}, f32[9,192,128]{2,1,0:T(8,128)}, u32[]{:S(2)}, u32[]{:S(2)}) collective-permute-start(f32[9,192,128]{2,1,0:T(8,128)} %collective-permute-done.14), channel_id=1, source_target_pairs={{0,1},{1,0},{2,3},{3,2},{4,5},{5,4},{6,7},{7,6},{8,9},{9,8},{10,11... | collective-permute-start | bytes 2654216 | tf_op jit(solution)/shard_map/ppermute | solution.py:32
  252.7 5.7 %collective-permute-start.11 = (f32[41216]{0:T(1024)S(1)}, f32[41216]{0:T(1024)S(1)}, u32[]{:S(2)}, u32[]{:S(2)}) collective-permute-start(f32[41216]{0:T(1024)S(1)} %add.113), channel_id=1, source_target_pairs={{0,32},{8,40},{16,48},{24,56},{32,0},{40,8},{48,16},{56,24},{64,96... | collective-permute-start | bytes 494600 | tf_op jit(solution)/shard_map/ppermute | solution.py:15
  258.4 9.6 %collective-permute-start.12 = (f32[41216]{0:T(1024)S(1)}, f32[41216]{0:T(1024)S(1)}, u32[]{:S(2)}, u32[]{:S(2)}) collective-permute-start(f32[41216]{0:T(1024)S(1)} %add.114), channel_id=1, source_target_pairs={{0,64},{8,72},{16,80},{24,88},{32,96},{40,104},{48,112},{56,120},{... | collective-permute-start | bytes 494600 | tf_op jit(solution)/shard_map/ppermute | solution.py:15
  261.5 41.3 %collective-permute-start.17 = (f32[9,192,128]{2,1,0:T(8,128)}, f32[9,192,128]{2,1,0:T(8,128)}, u32[]{:S(2)}, u32[]{:S(2)}) collective-permute-start(f32[9,192,128]{2,1,0:T(8,128)} %collective-permute-done.16), channel_id=1, source_target_pairs={{0,1},{1,0},{2,3},{3,2},{4,5},{5,4},{6,7},{7,6},{8,9},{9,8},{10,11... | collective-permute-start | bytes 2654216 | tf_op jit(solution)/shard_map/ppermute | solution.py:32
  268.1 15.2 %collective-permute-start.13 = (f32[41216]{0:T(1024)S(1)}, f32[41216]{0:T(1024)S(1)}, u32[]{:S(2)}, u32[]{:S(2)}) collective-permute-start(f32[41216]{0:T(1024)S(1)} %add.115), channel_id=1, source_target_pairs={{0,128},{8,136},{16,144},{24,152},{32,160},{40,168},{48,176},{56,1... | collective-permute-start | bytes 494600 | tf_op jit(solution)/shard_map/ppermute | solution.py:15
  317.3 10.9 %all-to-all-start.1 = ((f32[8,1,6912]{2,1,0:T(1,128)}), f32[8,1,6912]{2,1,0:T(1,128)S(1)}, u32[]{:S(2)}, u32[]{:S(2)}) async-start(f32[8,1,6912]{2,1,0:T(1,128)} %reshape.137), calls=%async_computation.1 | async-start | bytes 442368 | tf_op jit(solution)/shard_map/all_to_all | solution.py:83
  341.5 6.5 %collective-permute-start.19 = (f32[512,32]{0,1:T(8,128)S(1)}, f32[512,32]{0,1:T(8,128)S(1)}, u32[]{:S(2)}, u32[]{:S(2)}) collective-permute-start(f32[512,32]{0,1:T(8,128)S(1)} %add.123), channel_id=1, source_target_pairs={{0,16},{8,24},{16,0},{24,8},{32,48},{40,56},{48,32},{56,40},{64,80... | collective-permute-start | bytes 196616 | tf_op jit(solution)/shard_map/ppermute | solution.py:15
  352.4 5.5 %collective-permute-start.21 = (f32[512,32]{0,1:T(8,128)S(1)}, f32[512,32]{0,1:T(8,128)S(1)}, u32[]{:S(2)}, u32[]{:S(2)}) collective-permute-start(f32[512,32]{0,1:T(8,128)S(1)} %add.125), channel_id=1, source_target_pairs={{0,64},{8,72},{16,80},{24,88},{32,96},{40,104},{48,112},{56,120},{... | collective-permute-start | bytes 196616 | tf_op jit(solution)/shard_map/ppermute | solution.py:15
  358.0 8.3 %collective-permute-start.22 = (f32[512,32]{0,1:T(8,128)S(1)}, f32[512,32]{0,1:T(8,128)S(1)}, u32[]{:S(2)}, u32[]{:S(2)}) collective-permute-start(f32[512,32]{0,1:T(8,128)S(1)} %add.126), channel_id=1, source_target_pairs={{0,128},{8,136},{16,144},{24,152},{32,160},{40,168},{48,176},{56,1... | collective-permute-start | bytes 196616 | tf_op jit(solution)/shard_map/ppermute | solution.py:15
  (20 other events, 415.2 us)
Sparse Core Ops, SparseCore 0:
  9.8 31.0 all-gather.2
  181.7 27.7 all-gather.4

commit v3 on v2

--- a/solution.py
+++ b/solution.py
@@ -2,6 +2,7 @@
 import jax.numpy as jnp
 from jax import lax
 from jax.sharding import PartitionSpec as P
+
 
 CELLS = 9
 HIGHEST = lax.Precision.HIGHEST
@@ -45,26 +46,16 @@
     block_rows, neigh = local_ids.shape
     columns = jnp.arange(ext_blocks, dtype=jnp.int32)
     onehot = local_ids[:, :, None] == columns[None, None, :]
-    rows, cols = force_blocks.shape[2], force_blocks.shape[3]
-    table = force_blocks.reshape(block_rows, neigh, rows * cols)
-    picked = jnp.einsum(
-        "ikj,ikx->ijx",
-        onehot.astype(jnp.float32),
-        table,
-        precision=HIGHEST,
-        preferred_element_type=jnp.float32,
-    )
-    return picked.reshape(block_rows, ext_blocks, rows, cols)
+    offsets = jnp.arange(neigh, dtype=jnp.int32)
+    which = jnp.sum(jnp.where(onehot, offsets[None, :, None], 0), axis=1)
+    valid = jnp.any(onehot, axis=1)
+    picked = force_blocks[jnp.arange(block_rows, dtype=jnp.int32)[:, None], which]
+    return jnp.where(valid[:, :, None, None], picked, 0.0)
 
 
 def apply_dense(dense, low, own, high):
     width = low.shape[0]
     own_count = own.shape[0]
-    mode_count = lax.axis_size("mode")
-
-    def split(field):
-        return field.reshape(field.shape[0], field.shape[1], mode_count, -1)
-
     parts = (
         (dense[:, width : width + own_count], own),
         (dense[:, :width], low),
@@ -73,19 +64,18 @@
     total = None
     for coeffs, field in parts:
         product = jnp.einsum(
-            "ijrc,jcdm->dirm",
+            "ijrc,jcm->irm",
             coeffs,
-            split(field),
+            field,
             precision=HIGHEST,
             preferred_element_type=jnp.float32,
         )
         total = product if total is None else total + product
-    regrouped = lax.all_to_all(total, "mode", split_axis=0, concat_axis=0, tiled=True)
-    regrouped = jnp.transpose(regrouped, (1, 0, 2, 3))
-    return regrouped.reshape(-1, regrouped.shape[3])
+    regrouped = lax.all_to_all(total, "mode", split_axis=2, concat_axis=1, tiled=True)
+    return regrouped.reshape(-1, regrouped.shape[2])
 
 
-def local(vectors, force_blocks, inverse_blocks, neighbours):
+def staged(vectors, force_blocks, inverse_blocks, neighbours):
     row_count, col_count = vectors.shape
     block_size = inverse_blocks.shape[1]
     block_rows = row_count // block_size
@@ -198,4 +188,4 @@
         P(None, None, "mode"),
         P(None, None, "mode"),
     )
-    return jax.shard_map(local, mesh=mesh, in_specs=in_specs, out_specs=out_specs, check_vma=False)
+    return jax.shard_map(staged, mesh=mesh, in_specs=in_specs, out_specs=out_specs, check_vma=False)

time: 381 us -> 355 us (0.932)
  the two profiles are of different devices: /device:TPU:2 before, /device:TPU:8 now
where the time goes in v3:
time: 355 us; the launch traced here: 351 us
  waiting for transfers between devices  156 us (44%)
  local copies, waits for them, and re-layouts  79 us (22%)
  matrix products  44.4 us (13%)
  starting transfers between devices  37 us (10%)
  other arithmetic  19.1 us (5%)
  between operations  14.7 us (4%)
    ppermute x15, waiting for transfers between devices, space_sum(): value = value + lax.ppermute(value, 'space', pairs)  59.3 us
    ppermute x4, waiting for transfers between devices, send(): got = lax.ppermute(mine, 'space', pairs)  47.7 us
    all_gather x1, waiting for transfers between devices, staged(): full_x = lax.all_gather(stacked_x, 'mode', axis=2, tiled=True)  30.6 us
    dot_general x6, matrix products, apply_dense(): jnp.einsum('ijrc,jcm->irm', coeffs, field, precision=HIGHEST, preferred_e...  27.1 us
    unnamed x33, local copies, waits for them, and re-layouts  15.6 us
    ppermute x15, starting transfers between devices, space_sum(): value = value + lax.ppermute(value, 'space', pairs)  13.8 us
    all_gather x1, waiting for transfers between devices, staged(): full_s = lax.all_gather(search_raw, 'mode', axis=2, tiled=True)  12.5 us
    all_to_all x2, starting transfers between devices, apply_dense(): lax.all_to_all(total, 'mode', split_axis=2, concat_axis=1, tiled=True)  11.1 us
  transfers between devices with their start and end apart: 27, of which 19 were waited for; matrix products, arithmetic and copies ran while one was open for 18% of the time, Pallas kernels for 0%

profile of v3, /device:TPU:8, one launch (start us, length us, event | category | flops | bytes accessed | tf_op | source)
XLA Modules:
  0.0 350.5 jit_solution(13418464921398943115)
XLA Ops:
  9.4 30.6 %all-gather.3.cloned.1.call-done = f32[9,192,256]{1,2,0:T(8,128)} async-done(((f32[9,192,32]{1,2,0:T(8,128)}), f32[9,192,256]{1,2,0:T(8,128)}) %all-gather.3.cloned.1.call-update) | async-done | bytes 1769488 | tf_op jit(solution)/shard_map/all_gather | solution.py:95
  44.1 4.0 %collective-permute-start.2 = (f32[9,192,128]{2,1,0:T(8,128)}, f32[9,192,128]{2,1,0:T(8,128)S(1)}, u32[]{:S(2)}, u32[]{:S(2)}) collective-permute-start(f32[9,192,128]{2,1,0:T(8,128)} %copy.57), channel_id=1, source_target_pairs={{8,0},{16,8},{24,16},{32,24},{40,32},{48,40},{56,48},{64,56},{72,6... | collective-permute-start | bytes 2654216 | tf_op jit(solution)/shard_map/ppermute | solution.py:32
  48.1 20.4 %collective-permute-done = f32[9,192,128]{2,1,0:T(8,128)} collective-permute-done((f32[9,192,128]{2,1,0:T(8,128)}, f32[9,192,128]{2,1,0:T(8,128)}, u32[]{:S(2)}, u32[]{:S(2)}) %collective-permute-start) | collective-permute-done | bytes 884768 | tf_op jit(solution)/shard_map/ppermute | solution.py:32
  69.6 7.1 %gather_fusion = f32[243,24,192]{2,1,0:T(8,128)} fusion(f32[9,27,24,192]{3,2,1,0:T(8,128)} %param.5, s32[243]{0:T(256)S(1)} %reshape.100), kind=kCustom, calls=%fused_computation | custom fusion | bytes 8959896 | tf_op jit(solution)/shard_map/gather | solution.py:52
  76.8 4.7 %fusion.64 = f32[9,24,256]{2,1,0:T(8,128)S(1)} fusion(f32[9,192,256]{1,2,0:T(8,128)} %all-gather.3.cloned.1.call-done, f32[9,27,24,192]{3,2,1,0:T(8,128)} %bitcast.132, pred[9,27]{1,0:T(8,128)(4,1)S(1)} %fusion.117), kind=kOutput, calls=%fused_computation.66 | convolution fusion | flops 1147737600 | bytes 6469875 | tf_op jit(solution)/shard_map/ijrc,jcm->irm/dot_general | solution.py:66
  81.5 4.0 %fusion.94 = f32[9,24,256]{2,1,0:T(8,128)S(1)} fusion(f32[9,24,256]{2,1,0:T(8,128)S(1)} %fusion.64, f32[9,192,128]{2,1,0:T(8,128)} %collective-permute-done.1, f32[9,192,128]{2,1,0:T(8,128)} %collective-permute-done, f32[9,27,24,192]{3,2,1,0:T(8,128)S(1)} %bitcast.136, pred[9,27]{1,0:T(8,128)(4,1)S(1)} %fusion.117, pred[]{:T(512)S(6)} %eq.28), kind=kOutput, calls=%fused_computation.72 | convolution fusion | flops 1149120000 | bytes 6691060 | tf_op jit(solution)/shard_map/ijrc,jcm->irm/dot_general | solution.py:66
  94.5 5.4 %all-to-all-start = ((f32[8,1,6912]{2,1,0:T(1,128)}), f32[8,1,6912]{2,1,0:T(1,128)}, u32[]{:S(2)}, u32[]{:S(2)}) async-start(f32[8,1,6912]{2,1,0:T(1,128)} %reshape.121), calls=%async_computation | async-start | bytes 442368 | tf_op jit(solution)/shard_map/all_to_all | solution.py:74
  124.4 4.5 %collective-permute-done.5 = f32[256,32]{0,1:T(8,128)S(1)} collective-permute-done((f32[256,32]{0,1:T(8,128)S(1)}, f32[256,32]{0,1:T(8,128)S(1)}, u32[]{:S(2)}, u32[]{:S(2)}) %collective-permute-start.5) | collective-permute-done | bytes 32800 | tf_op jit(solution)/shard_map/ppermute | solution.py:16
  128.9 3.9 %collective-permute-done.6 = f32[256,32]{0,1:T(8,128)S(1)} collective-permute-done((f32[256,32]{0,1:T(8,128)S(1)}, f32[256,32]{0,1:T(8,128)S(1)}, u32[]{:S(2)}, u32[]{:S(2)}) %collective-permute-start.6) | collective-permute-done | bytes 32800 | tf_op jit(solution)/shard_map/ppermute | solution.py:16
  137.7 6.0 %collective-permute-start.8 = (f32[256,32]{0,1:T(8,128)S(1)}, f32[256,32]{0,1:T(8,128)S(1)}, u32[]{:S(2)}, u32[]{:S(2)}) collective-permute-start(f32[256,32]{0,1:T(8,128)S(1)} %add.122), channel_id=1, source_target_pairs={{0,128},{8,136},{16,144},{24,152},{32,160},{40,168},{48,176},{56,1... | collective-permute-start | bytes 98312 | tf_op jit(solution)/shard_map/ppermute | solution.py:16
  168.5 12.5 %all-gather.5.cloned.1.call-done = f32[9,192,256]{1,2,0:T(8,128)} async-done(((f32[9,192,32]{1,2,0:T(8,128)}), f32[9,192,256]{1,2,0:T(8,128)}) %all-gather.5.cloned.1.call-update) | async-done | bytes 1769488 | tf_op jit(solution)/shard_map/all_gather | solution.py:122
  200.1 4.8 %collective-permute-start.16 = (f32[9,192,128]{2,1,0:T(8,128)}, f32[9,192,128]{2,1,0:T(8,128)}, u32[]{:S(2)}, u32[]{:S(2)}) collective-permute-start(f32[9,192,128]{2,1,0:T(8,128)} %copy.68), channel_id=1, source_target_pairs={{8,0},{16,8},{24,16},{32,24},{40,32},{48,40},{56,48},{64,56},{72,6... | collective-permute-start | bytes 2654216 | tf_op jit(solution)/shard_map/ppermute | solution.py:32
  206.0 27.3 %collective-permute-done.14 = f32[9,192,128]{2,1,0:T(8,128)} collective-permute-done((f32[9,192,128]{2,1,0:T(8,128)}, f32[9,192,128]{2,1,0:T(8,128)}, u32[]{:S(2)}, u32[]{:S(2)}) %collective-permute-start.14) | collective-permute-done | bytes 884768 | tf_op jit(solution)/shard_map/ppermute | solution.py:32
  235.9 5.2 %collective-permute-done.11 = f32[41216]{0:T(1024)} collective-permute-done((f32[41216]{0:T(1024)}, f32[41216]{0:T(1024)}, u32[]{:S(2)}, u32[]{:S(2)}) %collective-permute-start.11) | collective-permute-done | bytes 164896 | tf_op jit(solution)/shard_map/ppermute | solution.py:16
  243.9 8.7 %collective-permute-done.12 = f32[41216]{0:T(1024)S(1)} collective-permute-done((f32[41216]{0:T(1024)S(1)}, f32[41216]{0:T(1024)S(1)}, u32[]{:S(2)}, u32[]{:S(2)}) %collective-permute-start.12) | collective-permute-done | bytes 164896 | tf_op jit(solution)/shard_map/ppermute | solution.py:16
  253.0 5.2 %fusion.59 = f32[9,24,256]{2,1,0:T(8,128)} fusion(f32[9,192,256]{1,2,0:T(8,128)} %all-gather.5.cloned.1.call-done, f32[9,27,24,192]{3,2,1,0:T(8,128)} %bitcast.133, pred[9,27]{1,0:T(8,128)(4,1)S(1)} %fusion.117), kind=kOutput, calls=%fused_computation.65 | convolution fusion | flops 1147737600 | bytes 6469875 | tf_op jit(solution)/shard_map/ijrc,jcm->irm/dot_general | solution.py:66
  258.2 5.4 %collective-permute-done.13 = f32[41216]{0:T(1024)S(1)} collective-permute-done((f32[41216]{0:T(1024)S(1)}, f32[41216]{0:T(1024)S(1)}, u32[]{:S(2)}, u32[]{:S(2)}) %collective-permute-start.13) | collective-permute-done | bytes 164896 | tf_op jit(solution)/shard_map/ppermute | solution.py:16
  268.7 4.6 %fusion.104 = f32[9,24,256]{2,1,0:T(8,128)S(1)} fusion(f32[9,24,256]{2,1,0:T(8,128)} %fusion.59, f32[9,192,128]{2,1,0:T(8,128)} %collective-permute-done.15, f32[9,192,128]{2,1,0:T(8,128)} %collective-permute-done.14, f32[9,27,24,192]{3,2,1,0:T(8,128)} %bitcast.134, pred[9,27]{1,0:T(8,128)(4,1)S(1)} %fusion.117, pred[]{:T(512)S(6)} %eq.28), kind=kOutput, calls=%fused_computation.74 | convolution fusion | flops 1149120000 | bytes 6691060 | tf_op jit(solution)/shard_map/ijrc,jcm->irm/dot_general | solution.py:66
  273.3 5.2 %fusion.99 = f32[9,24,256]{2,1,0:T(8,128)} fusion(f32[9,24,256]{2,1,0:T(8,128)S(1)} %fusion.104, f32[9,192,128]{2,1,0:T(8,128)} %collective-permute-done.17, f32[9,192,128]{2,1,0:T(8,128)} %collective-permute-done.16, f32[9,27,24,192]{3,2,1,0:T(8,128)} %bitcast.135, pred[9,27]{1,0:T(8,128)(4,1)S(1)} %fusion.117, pred[]{:T(512)S(6)} %eq.28), kind=kOutput, calls=%fused_computation.73 | convolution fusion | flops 1149120000 | bytes 6691060 | tf_op jit(solution)/shard_map/ijrc,jcm->irm/dot_general | solution.py:66
  285.0 5.7 %all-to-all-start.1 = ((f32[8,1,6912]{2,1,0:T(1,128)}), f32[8,1,6912]{2,1,0:T(1,128)}, u32[]{:S(2)}, u32[]{:S(2)}) async-start(f32[8,1,6912]{2,1,0:T(1,128)} %reshape.123), calls=%async_computation.1 | async-start | bytes 442368 | tf_op jit(solution)/shard_map/all_to_all | solution.py:74
  311.8 4.4 %collective-permute-done.18 = f32[512,32]{0,1:T(8,128)S(1)} collective-permute-done((f32[512,32]{0,1:T(8,128)S(1)}, f32[512,32]{0,1:T(8,128)S(1)}, u32[]{:S(2)}, u32[]{:S(2)}) %collective-permute-start.18) | collective-permute-done | bytes 65568 | tf_op jit(solution)/shard_map/ppermute | solution.py:16
  322.3 4.8 %collective-permute-done.20 = f32[512,32]{0,1:T(8,128)S(1)} collective-permute-done((f32[512,32]{0,1:T(8,128)S(1)}, f32[512,32]{0,1:T(8,128)S(1)}, u32[]{:S(2)}, u32[]{:S(2)}) %collective-permute-start.20) | collective-permute-done | bytes 65568 | tf_op jit(solution)/shard_map/ppermute | solution.py:16
  327.6 6.1 %collective-permute-done.21 = f32[512,32]{0,1:T(8,128)S(1)} collective-permute-done((f32[512,32]{0,1:T(8,128)S(1)}, f32[512,32]{0,1:T(8,128)S(1)}, u32[]{:S(2)}, u32[]{:S(2)}) %collective-permute-start.21) | collective-permute-done | bytes 65568 | tf_op jit(solution)/shard_map/ppermute | solution.py:16
  336.5 5.5 %collective-permute-done.22 = f32[512,32]{0,1:T(8,128)S(1)} collective-permute-done((f32[512,32]{0,1:T(8,128)S(1)}, f32[512,32]{0,1:T(8,128)S(1)}, u32[]{:S(2)}, u32[]{:S(2)}) %collective-permute-start.22) | collective-permute-done | bytes 65568 | tf_op jit(solution)/shard_map/ppermute | solution.py:16
  (142 shorter events, 140.0 us)
Async XLA Ops:
  7.2 32.8 %all-gather.3.cloned.1.call-start = ((), (), s32[]{:S(2)}) async-start(), calls=%async_computation.2 | async-start | bytes 2654208 | tf_op jit(solution)/shard_map/all_gather | solution.py:95
  42.6 25.8 %collective-permute-start = (f32[9,192,128]{2,1,0:T(8,128)}, f32[9,192,128]{2,1,0:T(8,128)}, u32[]{:S(2)}, u32[]{:S(2)}) collective-permute-start(f32[9,192,128]{2,1,0:T(8,128)} %copy.57), channel_id=1, source_target_pairs={{0,8},{8,16},{16,24},{24,32},{32,40},{40,48},{48,56},{56,64},{64,7... | collective-permute-start | bytes 2654216 | tf_op jit(solution)/shard_map/ppermute | solution.py:32
  44.1 24.5 %collective-permute-start.2 = (f32[9,192,128]{2,1,0:T(8,128)}, f32[9,192,128]{2,1,0:T(8,128)S(1)}, u32[]{:S(2)}, u32[]{:S(2)}) collective-permute-start(f32[9,192,128]{2,1,0:T(8,128)} %copy.57), channel_id=1, source_target_pairs={{8,0},{16,8},{24,16},{32,24},{40,32},{48,40},{56,48},{64,56},{72,6... | collective-permute-start | bytes 2654216 | tf_op jit(solution)/shard_map/ppermute | solution.py:32
  68.4 13.1 %collective-permute-start.1 = (f32[9,192,128]{2,1,0:T(8,128)}, f32[9,192,128]{2,1,0:T(8,128)}, u32[]{:S(2)}, u32[]{:S(2)}) collective-permute-start(f32[9,192,128]{2,1,0:T(8,128)} %collective-permute-done), channel_id=1, source_target_pairs={{0,1},{1,0},{2,3},{3,2},{4,5},{5,4},{6,7},{7,6},{8,9},{9,8},{10,11... | collective-permute-start | bytes 2654216 | tf_op jit(solution)/shard_map/ppermute | solution.py:33
  68.6 16.9 %collective-permute-start.3 = (f32[9,192,128]{2,1,0:T(8,128)S(1)}, f32[9,192,128]{2,1,0:T(8,128)}, u32[]{:S(2)}, u32[]{:S(2)}) collective-permute-start(f32[9,192,128]{2,1,0:T(8,128)S(1)} %collective-permute-done.2), channel_id=1, source_target_pairs={{0,1},{1,0},{2,3},{3,2},{4,5},{5,4},{6,7},{7,6},{8,9},{9,8},{10,11... | collective-permute-start | bytes 2654216 | tf_op jit(solution)/shard_map/ppermute | solution.py:33
  94.5 11.1 %all-to-all-start = ((f32[8,1,6912]{2,1,0:T(1,128)}), f32[8,1,6912]{2,1,0:T(1,128)}, u32[]{:S(2)}, u32[]{:S(2)}) async-start(f32[8,1,6912]{2,1,0:T(1,128)} %reshape.121), calls=%async_computation | async-start | bytes 442368 | tf_op jit(solution)/shard_map/all_to_all | solution.py:74
  99.9 81.1 %all-gather.5.cloned.1.call-start = ((), (), s32[]{:S(2)}) async-start(), calls=%async_computation.3 | async-start | bytes 2654208 | tf_op jit(solution)/shard_map/all_gather | solution.py:122
  123.5 5.4 %collective-permute-start.5 = (f32[256,32]{0,1:T(8,128)S(1)}, f32[256,32]{0,1:T(8,128)S(1)}, u32[]{:S(2)}, u32[]{:S(2)}) collective-permute-start(f32[256,32]{0,1:T(8,128)S(1)} %add.119), channel_id=1, source_target_pairs={{0,16},{8,24},{16,0},{24,8},{32,48},{40,56},{48,32},{56,40},{64,80... | collective-permute-start | bytes 98312 | tf_op jit(solution)/shard_map/ppermute | solution.py:16
  132.9 4.8 %collective-permute-start.7 = (f32[256,32]{0,1:T(8,128)S(1)}, f32[256,32]{0,1:T(8,128)S(1)}, u32[]{:S(2)}, u32[]{:S(2)}) collective-permute-start(f32[256,32]{0,1:T(8,128)S(1)} %add.121), channel_id=1, source_target_pairs={{0,64},{8,72},{16,80},{24,88},{32,96},{40,104},{48,112},{56,120},{... | collective-permute-start | bytes 98312 | tf_op jit(solution)/shard_map/ppermute | solution.py:16
  137.7 8.2 %collective-permute-start.8 = (f32[256,32]{0,1:T(8,128)S(1)}, f32[256,32]{0,1:T(8,128)S(1)}, u32[]{:S(2)}, u32[]{:S(2)}) collective-permute-start(f32[256,32]{0,1:T(8,128)S(1)} %add.122), channel_id=1, source_target_pairs={{0,128},{8,136},{16,144},{24,152},{32,160},{40,168},{48,176},{56,1... | collective-permute-start | bytes 98312 | tf_op jit(solution)/shard_map/ppermute | solution.py:16
  194.9 9.9 %collective-permute-start.9 = (f32[41216]{0:T(1024)}, f32[41216]{0:T(1024)}, u32[]{:S(2)}, u32[]{:S(2)}) collective-permute-start(f32[41216]{0:T(1024)} %pad_maximum_fusion.1), channel_id=1, source_target_pairs={{0,8},{8,0},{16,24},{24,16},{32,40},{40,32},{48,56},{56,48},{64,72... | collective-permute-start | bytes 494600 | tf_op jit(solution)/shard_map/ppermute | solution.py:16
  200.1 42.1 %collective-permute-start.16 = (f32[9,192,128]{2,1,0:T(8,128)}, f32[9,192,128]{2,1,0:T(8,128)}, u32[]{:S(2)}, u32[]{:S(2)}) collective-permute-start(f32[9,192,128]{2,1,0:T(8,128)} %copy.68), channel_id=1, source_target_pairs={{8,0},{16,8},{24,16},{32,24},{40,32},{48,40},{56,48},{64,56},{72,6... | collective-permute-start | bytes 2654216 | tf_op jit(solution)/shard_map/ppermute | solution.py:32
  204.9 28.5 %collective-permute-start.14 = (f32[9,192,128]{2,1,0:T(8,128)}, f32[9,192,128]{2,1,0:T(8,128)}, u32[]{:S(2)}, u32[]{:S(2)}) collective-permute-start(f32[9,192,128]{2,1,0:T(8,128)} %copy.68), channel_id=1, source_target_pairs={{0,8},{8,16},{16,24},{24,32},{32,40},{40,48},{48,56},{56,64},{64,7... | collective-permute-start | bytes 2654216 | tf_op jit(solution)/shard_map/ppermute | solution.py:32
  205.9 27.4 %collective-permute-start.10 = (f32[41216]{0:T(1024)S(1)}, f32[41216]{0:T(1024)S(1)}, u32[]{:S(2)}, u32[]{:S(2)}) collective-permute-start(f32[41216]{0:T(1024)S(1)} %fusion.147), channel_id=1, source_target_pairs={{0,16},{8,24},{16,0},{24,8},{32,48},{40,56},{48,32},{56,40},{64,80... | collective-permute-start | bytes 494600 | tf_op jit(solution)/shard_map/ppermute | solution.py:16
  233.3 35.4 %collective-permute-start.15 = (f32[9,192,128]{2,1,0:T(8,128)}, f32[9,192,128]{2,1,0:T(8,128)}, u32[]{:S(2)}, u32[]{:S(2)}) collective-permute-start(f32[9,192,128]{2,1,0:T(8,128)} %collective-permute-done.14), channel_id=1, source_target_pairs={{0,1},{1,0},{2,3},{3,2},{4,5},{5,4},{6,7},{7,6},{8,9},{9,8},{10,11... | collective-permute-start | bytes 2654216 | tf_op jit(solution)/shard_map/ppermute | solution.py:33
  234.0 7.0 %collective-permute-start.11 = (f32[41216]{0:T(1024)}, f32[41216]{0:T(1024)}, u32[]{:S(2)}, u32[]{:S(2)}) collective-permute-start(f32[41216]{0:T(1024)} %add.125), channel_id=1, source_target_pairs={{0,32},{8,40},{16,48},{24,56},{32,0},{40,8},{48,16},{56,24},{64,96... | collective-permute-start | bytes 494600 | tf_op jit(solution)/shard_map/ppermute | solution.py:16
  242.1 10.5 %collective-permute-start.12 = (f32[41216]{0:T(1024)S(1)}, f32[41216]{0:T(1024)S(1)}, u32[]{:S(2)}, u32[]{:S(2)}) collective-permute-start(f32[41216]{0:T(1024)S(1)} %add.126), channel_id=1, source_target_pairs={{0,64},{8,72},{16,80},{24,88},{32,96},{40,104},{48,112},{56,120},{... | collective-permute-start | bytes 494600 | tf_op jit(solution)/shard_map/ppermute | solution.py:16
  242.2 31.1 %collective-permute-start.17 = (f32[9,192,128]{2,1,0:T(8,128)}, f32[9,192,128]{2,1,0:T(8,128)}, u32[]{:S(2)}, u32[]{:S(2)}) collective-permute-start(f32[9,192,128]{2,1,0:T(8,128)} %collective-permute-done.16), channel_id=1, source_target_pairs={{0,1},{1,0},{2,3},{3,2},{4,5},{5,4},{6,7},{7,6},{8,9},{9,8},{10,11... | collective-permute-start | bytes 2654216 | tf_op jit(solution)/shard_map/ppermute | solution.py:33
  252.6 10.9 %collective-permute-start.13 = (f32[41216]{0:T(1024)S(1)}, f32[41216]{0:T(1024)S(1)}, u32[]{:S(2)}, u32[]{:S(2)}) collective-permute-start(f32[41216]{0:T(1024)S(1)} %add.127), channel_id=1, source_target_pairs={{0,128},{8,136},{16,144},{24,152},{32,160},{40,168},{48,176},{56,1... | collective-permute-start | bytes 494600 | tf_op jit(solution)/shard_map/ppermute | solution.py:16
  285.0 11.4 %all-to-all-start.1 = ((f32[8,1,6912]{2,1,0:T(1,128)}), f32[8,1,6912]{2,1,0:T(1,128)}, u32[]{:S(2)}, u32[]{:S(2)}) async-start(f32[8,1,6912]{2,1,0:T(1,128)} %reshape.123), calls=%async_computation.1 | async-start | bytes 442368 | tf_op jit(solution)/shard_map/all_to_all | solution.py:74
  316.2 5.9 %collective-permute-start.19 = (f32[512,32]{0,1:T(8,128)S(1)}, f32[512,32]{0,1:T(8,128)S(1)}, u32[]{:S(2)}, u32[]{:S(2)}) collective-permute-start(f32[512,32]{0,1:T(8,128)S(1)} %add.134), channel_id=1, source_target_pairs={{0,16},{8,24},{16,0},{24,8},{32,48},{40,56},{48,32},{56,40},{64,80... | collective-permute-start | bytes 196616 | tf_op jit(solution)/shard_map/ppermute | solution.py:16
  322.1 5.1 %collective-permute-start.20 = (f32[512,32]{0,1:T(8,128)S(1)}, f32[512,32]{0,1:T(8,128)S(1)}, u32[]{:S(2)}, u32[]{:S(2)}) collective-permute-start(f32[512,32]{0,1:T(8,128)S(1)} %add.135), channel_id=1, source_target_pairs={{0,32},{8,40},{16,48},{24,56},{32,0},{40,8},{48,16},{56,24},{64,96... | collective-permute-start | bytes 196616 | tf_op jit(solution)/shard_map/ppermute | solution.py:16
  327.1 6.6 %collective-permute-start.21 = (f32[512,32]{0,1:T(8,128)S(1)}, f32[512,32]{0,1:T(8,128)S(1)}, u32[]{:S(2)}, u32[]{:S(2)}) collective-permute-start(f32[512,32]{0,1:T(8,128)S(1)} %add.136), channel_id=1, source_target_pairs={{0,64},{8,72},{16,80},{24,88},{32,96},{40,104},{48,112},{56,120},{... | collective-permute-start | bytes 196616 | tf_op jit(solution)/shard_map/ppermute | solution.py:16
  333.7 8.3 %collective-permute-start.22 = (f32[512,32]{0,1:T(8,128)S(1)}, f32[512,32]{0,1:T(8,128)S(1)}, u32[]{:S(2)}, u32[]{:S(2)}) collective-permute-start(f32[512,32]{0,1:T(8,128)S(1)} %add.137), channel_id=1, source_target_pairs={{0,128},{8,136},{16,144},{24,152},{32,160},{40,168},{48,176},{56,1... | collective-permute-start | bytes 196616 | tf_op jit(solution)/shard_map/ppermute | solution.py:16
  (15 other events, 341.5 us)
Sparse Core Ops, SparseCore 0:
  9.8 30.0 all-gather.2
  154.3 26.7 all-gather.4
